TPU v7x, 1024 devices: a whole 4x4x32 slice. The times are simulated.
1024 devices in a mesh: ctx: 128 (over y, z), head: 8 (over x, core).
Axes of the slice: x: 4, y: 4, z: 32, core: 2. Of those that a mesh axis runs over, the one named last changes fastest.
Arguments:
- query_rows: bfloat16 [16384, 2048], P('ctx', 'head'), may hold values from -40 to 40
- key_rows: bfloat16 [16384, 2048], P('ctx', 'head'), may hold values from -6 to 6
- value_rows: bfloat16 [16384, 2048], P('ctx', 'head'), may hold values from -40 to 40
- norm_gain: bfloat16 [2048], P('head'), may hold values from 0.099609375 to 1.8984375
- cotangent: bfloat16 [16384, 2048], P('ctx', 'head'), may hold values from -6 to 6
Outputs:
- normed: bfloat16 [16384, 2048], P('ctx', 'head')
- query_grad: bfloat16 [16384, 2048], P('ctx', 'head')
- key_grad: bfloat16 [16384, 2048], P('ctx', 'head')
- value_grad: bfloat16 [16384, 2048], P('ctx', 'head')
All inputs are finite; a program needn't handle non-finite values.
Results may differ from a plain program's by a relative error of at most 0.0058.
Values sent between devices are 32-bit elements; how exact they have to be, the bound alone decides.
No kernel may reach another device: no remote copies, remote signals or barrier semaphores. Data moves between devices by JAX's collectives and lax.ppermute only.
A program may use at most 64 MiB of HBM per device.

v0:
```python
import jax
import jax.numpy as jnp
from jax import lax
from jax.sharding import PartitionSpec as P

HEADS = 32
HEAD_DIM = 64


EPS = 1e-05


def prefix(value, axis, combine, identity, reverse):
    peers, position = (lax.axis_size(axis), lax.axis_index(axis))
    everything = lax.all_gather(value, axis)
    start = jnp.broadcast_to(jnp.asarray(identity, value.dtype), value.shape)

    def hop(k, before):
        at = peers - 1 - k if reverse else k
        reached = at > position if reverse else at < position
        new = combine(before, everything[at])
        return jnp.where(reached, new, before)

    return lax.fori_loop(0, peers, hop, start)


def add_states(earlier, later):
    return earlier + later


def on_device(query_rows, key_rows, value_rows, norm_gain, cotangent):
    tokens_here = query_rows.shape[0]
    heads_here = query_rows.shape[1] // HEAD_DIM
    width_all = HEADS * HEAD_DIM

    def split_heads(array):
        return array.reshape(tokens_here, heads_here, HEAD_DIM)

    queries = split_heads(query_rows)
    key_local = split_heads(key_rows)
    value_local = split_heads(value_rows)
    gain = norm_gain.astype(jnp.float32)
    causal = lax.broadcasted_iota(jnp.int32, (tokens_here, tokens_here), 0) >= lax.broadcasted_iota(
        jnp.int32, (tokens_here, tokens_here), 1
    )
    local_state = jnp.einsum(
        "thd,the->hde", key_local, value_local, preferred_element_type=jnp.float32
    )
    empty_state = jnp.zeros_like(local_state)
    carried = prefix(local_state, "ctx", add_states, empty_state, False)
    carried_bf = carried.astype(jnp.bfloat16)
    scores = jnp.einsum("thd,shd->hts", queries, key_local, preferred_element_type=jnp.float32)
    masked = jnp.where(causal[None], scores, 0.0).astype(jnp.bfloat16)
    attended = jnp.einsum("hts,shd->thd", masked, value_local, preferred_element_type=jnp.float32)
    attended = attended + jnp.einsum(
        "thd,hde->the", queries, carried_bf, preferred_element_type=jnp.float32
    )
    flat = attended.reshape(tokens_here, heads_here * HEAD_DIM)
    square_local = jnp.sum(flat * flat, axis=1)
    upstream = cotangent.astype(jnp.float32) * gain
    inner_local = jnp.sum(upstream * flat, axis=1)
    square_all = lax.psum(square_local, "head")
    recip = lax.rsqrt(square_all / width_all + EPS)
    normed = (flat * recip[:, None] * gain).astype(jnp.bfloat16)
    inner_all = lax.psum(inner_local, "head")
    grad_flat = (
        recip[:, None] * upstream - flat * (recip * recip * recip * inner_all / width_all)[:, None]
    )
    grad_out = split_heads(grad_flat.astype(jnp.bfloat16))
    grad_scores = jnp.einsum(
        "thd,shd->hts", grad_out, value_local, preferred_element_type=jnp.float32
    )
    grad_masked = jnp.where(causal[None], grad_scores, 0.0).astype(jnp.bfloat16)
    query_grad = jnp.einsum(
        "hts,shd->thd", grad_masked, key_local, preferred_element_type=jnp.float32
    )
    query_grad = query_grad + jnp.einsum(
        "the,hde->thd", grad_out, carried_bf, preferred_element_type=jnp.float32
    )
    local_grad = jnp.einsum("thd,the->hde", queries, grad_out, preferred_element_type=jnp.float32)
    later = prefix(local_grad, "ctx", add_states, empty_state, True)
    later_bf = later.astype(jnp.bfloat16)
    key_grad = jnp.einsum("hts,thd->shd", grad_masked, queries, preferred_element_type=jnp.float32)
    key_grad = key_grad + jnp.einsum(
        "she,hde->shd", value_local, later_bf, preferred_element_type=jnp.float32
    )
    value_grad = jnp.einsum("hts,thd->shd", masked, grad_out, preferred_element_type=jnp.float32)
    value_grad = value_grad + jnp.einsum(
        "shd,hde->she", key_local, later_bf, preferred_element_type=jnp.float32
    )
    shape = (tokens_here, heads_here * HEAD_DIM)
    return (
        normed,
        query_grad.reshape(shape).astype(jnp.bfloat16),
        key_grad.reshape(shape).astype(jnp.bfloat16),
        value_grad.reshape(shape).astype(jnp.bfloat16),
    )


def solution(mesh):
    placed = (P("ctx", "head"), P("ctx", "head"), P("ctx", "head"), P("head"), P("ctx", "head"))
    return jax.shard_map(
        on_device,
        mesh=mesh,
        in_specs=placed,
        out_specs=(P("ctx", "head"), P("ctx", "head"), P("ctx", "head"), P("ctx", "head")),
        check_vma=False,
    )
```

profile of v0, /device:TPU:2, one launch (start us, length us, event | category | flops | bytes accessed | tf_op | source)
XLA Modules:
  0.0 897.4 jit_solution(8649496580436582443)
XLA Ops:
  8.2 1.0 copy.47
  13.1 315.1 %all-gather.5.cloned.1.call-done = f32[512,64,64]{2,1,0:T(8,128)} async-done(((f32[4,64,64]{2,1,0:T(8,128)}), f32[512,64,64]{2,1,0:T(8,128)}) %all-gather.5.cloned.1.call-update) | async-done | bytes 8388624 | tf_op jit(solution)/shard_map/all_gather | solution.py:15
  328.2 124.9 %while.30 = (s32[]{:T(128)}, f32[4,64,64]{2,1,0:T(8,128)S(1)}, s32[]{:T(128)}, f32[128,4,64,64]{3,2,1,0:T(8,128)}, s32[]{:T(128)}, /*index=5*/s32[]{:T(128)}) while((s32[]{:T(128)}, f32[4,64,64]{2,1,0:T(8,128)S(1)}, s32[]{:T(128)}, f32[128,4,64,64]{3,2,1,0:T(8,128)}, s32[]{:T(128)}, /*index=5*/s32[]{:T(128)}) %tuple.90), condition=%wide.region_1.2_spmd.clone, body=%wide.region_0.1_spmd.clone.sunk | while | flops 49156 | bytes 196701 | solution.py:24
  330.1 1.0 add_select_fusion.4
  332.1 1.0 add_select_fusion.4
  334.0 1.0 add_select_fusion.4
  336.0 1.0 add_select_fusion.4
  337.9 1.0 add_select_fusion.4
  339.9 1.0 add_select_fusion.4
  341.8 1.0 add_select_fusion.4
  342.8 1.0 add_select_fusion.4
  343.8 1.0 add_select_fusion.4
  344.7 1.0 add_select_fusion.4
  346.7 1.0 add_select_fusion.4
  348.6 1.0 add_select_fusion.4
  350.6 1.0 add_select_fusion.4
  352.5 1.0 add_select_fusion.4
  354.5 1.0 add_select_fusion.4
  356.4 1.0 add_select_fusion.4
  358.4 1.0 add_select_fusion.4
  360.4 1.0 add_select_fusion.4
  453.4 10.0 %all-reduce = (f32[128]{0:T(128)S(1)}, f32[128]{0:T(128)S(1)}) all-reduce(f32[128]{0:T(128)S(1)} %get-tuple-element.267, f32[128]{0:T(128)S(1)} %fusion.10), channel_id=1, replica_groups=mesh['ctx'=128,'head'=8] {'head'}, use_global_device_ids=true, to_apply=%region_3.4 | all-reduce | flops 256 | bytes 2048 | tf_op jit(solution)/shard_map/psum | solution.py:62
  466.7 296.1 %all-gather.7.cloned.1.call-done = f32[512,64,64]{2,1,0:T(8,128)} async-done(((f32[4,64,64]{2,1,0:T(8,128)}), f32[512,64,64]{2,1,0:T(8,128)}) %all-gather.7.cloned.1.call-update) | async-done | bytes 8388624 | tf_op jit(solution)/shard_map/all_gather | solution.py:15
  762.8 125.7 %while.31 = (s32[]{:T(128)}, f32[4,64,64]{2,1,0:T(8,128)S(1)}, s32[]{:T(128)}, f32[128,4,64,64]{3,2,1,0:T(8,128)}, s32[]{:T(128)}, /*index=5*/s32[]{:T(128)}, s32[]{:T(128)}, s32[]{:T(128)}) while((s32[]{:T(128)}, f32[4,64,64]{2,1,0:T(8,128)S(1)}, s32[]{:T(128)}, f32[128,4,64,64]{3,2,1,0:T(8,128)}, s32[]{:T(128)}, ...), condition=%wide.region_7.8_spmd.clone, body=%wide.region_6.7_spmd.clone.sunk | while | flops 49160 | bytes 196763 | solution.py:24
  (269 shorter events, 237.2 us)
Async XLA Ops:
  7.2 321.0 %all-gather.5.cloned.1.call-start = ((), (), s32[]{:S(2)}) async-start(), calls=%async_computation | async-start | bytes 16908288 | tf_op jit(solution)/shard_map/all_gather | solution.py:15
  10.0 752.8 %all-gather.7.cloned.1.call-start = ((), (), s32[]{:S(2)}) async-start(), calls=%async_computation.1 | async-start | bytes 16908288 | tf_op jit(solution)/shard_map/all_gather | solution.py:15
Sparse Core Ops, SparseCore 0:
  12.1 315.9 all-gather.4
  464.6 298.1 all-gather.6
where the time goes:
time: 902 us; the launch traced here: 897 us
  waiting for transfers between devices  611 us (68%)
  other arithmetic  245 us (27%)
  between operations  14.2 us (2%)
  blocking collectives  10 us (1%)
    all_gather x2, waiting for transfers between devices, prefix(): everything = lax.all_gather(value, axis)  611 us
    select_n x256, other arithmetic, hop(): return jnp.where(reached, new, before)  244 us
  transfers between devices with their start and end apart: 2, of which 2 were waited for; matrix products, arithmetic and copies ran while one was open for 1% of the time, Pallas kernels for 0%

commit v1 on v0

--- a/solution.py
+++ b/solution.py
@@ -10,22 +10,18 @@
 EPS = 1e-05
 
 
-def prefix(value, axis, combine, identity, reverse):
-    peers, position = (lax.axis_size(axis), lax.axis_index(axis))
-    everything = lax.all_gather(value, axis)
-    start = jnp.broadcast_to(jnp.asarray(identity, value.dtype), value.shape)
-
-    def hop(k, before):
-        at = peers - 1 - k if reverse else k
-        reached = at > position if reverse else at < position
-        new = combine(before, everything[at])
-        return jnp.where(reached, new, before)
-
-    return lax.fori_loop(0, peers, hop, start)
-
-
-def add_states(earlier, later):
-    return earlier + later
+def prefix(value, axis, reverse):
+    peers = lax.axis_size(axis)
+    rows = value.reshape(peers, -1)
+    mine = lax.all_to_all(rows, axis, 0, 0, tiled=True)
+    if reverse:
+        mine = mine[::-1]
+    shifted = jnp.concatenate([jnp.zeros_like(mine[:1]), mine[:-1]], axis=0)
+    total = jnp.cumsum(shifted, axis=0)
+    if reverse:
+        total = total[::-1]
+    back = lax.all_to_all(total, axis, 0, 0, tiled=True)
+    return lax.optimization_barrier(back).reshape(value.shape)
 
 
 def on_device(query_rows, key_rows, value_rows, norm_gain, cotangent):
@@ -46,8 +42,7 @@
     local_state = jnp.einsum(
         "thd,the->hde", key_local, value_local, preferred_element_type=jnp.float32
     )
-    empty_state = jnp.zeros_like(local_state)
-    carried = prefix(local_state, "ctx", add_states, empty_state, False)
+    carried = prefix(local_state, "ctx", False)
     carried_bf = carried.astype(jnp.bfloat16)
     scores = jnp.einsum("thd,shd->hts", queries, key_local, preferred_element_type=jnp.float32)
     masked = jnp.where(causal[None], scores, 0.0).astype(jnp.bfloat16)
@@ -78,7 +73,7 @@
         "the,hde->thd", grad_out, carried_bf, preferred_element_type=jnp.float32
     )
     local_grad = jnp.einsum("thd,the->hde", queries, grad_out, preferred_element_type=jnp.float32)
-    later = prefix(local_grad, "ctx", add_states, empty_state, True)
+    later = prefix(local_grad, "ctx", True)
     later_bf = later.astype(jnp.bfloat16)
     key_grad = jnp.einsum("hts,thd->shd", grad_masked, queries, preferred_element_type=jnp.float32)
     key_grad = key_grad + jnp.einsum(

time: 902 us -> 177 us (0.20)
  the two profiles are of different devices: /device:TPU:2 before, /device:TPU:32 now
where the time goes in v1:
time: 177 us; the launch traced here: 176 us
  waiting for transfers between devices  99.9 us (56%)
  starting transfers between devices  52 us (29%)
  blocking collectives  12.4 us (7%)
  local copies, waits for them, and re-layouts  7.98 us (5%)
  matrix products  2.18 us (1%)
    all_to_all x2, waiting for transfers between devices, prefix(): mine = lax.all_to_all(rows, axis, 0, 0, tiled=True)  51.3 us
    all_to_all x2, waiting for transfers between devices, prefix(): back = lax.all_to_all(total, axis, 0, 0, tiled=True)  48.6 us
    all_to_all x2, starting transfers between devices, prefix(): mine = lax.all_to_all(rows, axis, 0, 0, tiled=True)  39.3 us
    all_to_all x2, starting transfers between devices, prefix(): back = lax.all_to_all(total, axis, 0, 0, tiled=True)  12.8 us
    psum x1, blocking collectives, on_device(): square_all = lax.psum(square_local, 'head')  12.4 us
    unnamed x17, local copies, waits for them, and re-layouts  5.57 us
  transfers between devices with their start and end apart: 4, of which 4 were waited for; matrix products, arithmetic and copies ran while one was open for 2% of the time, Pallas kernels for 0%

profile of v1, /device:TPU:32, one launch (start us, length us, event | category | flops | bytes accessed | tf_op | source)
XLA Modules:
  0.0 176.5 jit_solution(16916703423262254084)
XLA Ops:
  0.6 1.0 copy.47
  1.9 0.7 all_to_all.26
  2.6 32.5 %all-to-all-start = ((f32[128,1,128]{2,1,0:T(1,128)}), f32[128,1,128]{2,1,0:T(1,128)S(1)}, u32[]{:S(2)}, u32[]{:S(2)}) async-start(f32[128,1,128]{2,1,0:T(1,128)} %bitcast.4), calls=%async_computation | async-start | bytes 131072 | tf_op jit(solution)/shard_map/all_to_all | solution.py:16
  35.3 0.7 copy-done.2
  36.2 0.5 copy-done.3
  36.7 25.0 %all-to-all-done = f32[128,1,128]{2,1,0:T(1,128)S(1)} async-done(((f32[128,1,128]{2,1,0:T(1,128)}), f32[128,1,128]{2,1,0:T(1,128)S(1)}, u32[]{:S(2)}, u32[]{:S(2)}) %all-to-all-start) | async-done | bytes 65568 | tf_op jit(solution)/shard_map/all_to_all | solution.py:16
  61.7 0.8 fusion.13
  62.5 6.4 %all-to-all-start.1 = ((f32[128,1,128]{2,1,0:T(1,128)}), f32[128,1,128]{2,1,0:T(1,128)S(1)}, u32[]{:S(2)}, u32[]{:S(2)}) async-start(f32[128,1,128]{2,1,0:T(1,128)} %fusion.13), calls=%async_computation.1 | async-start | bytes 131072 | tf_op jit(solution)/shard_map/all_to_all | solution.py:23
  68.9 0.2 fusion
  69.3 25.1 %all-to-all-done.1 = f32[128,1,128]{2,1,0:T(1,128)S(1)} async-done(((f32[128,1,128]{2,1,0:T(1,128)}), f32[128,1,128]{2,1,0:T(1,128)S(1)}, u32[]{:S(2)}, u32[]{:S(2)}) %all-to-all-start.1) | async-done | bytes 65568 | tf_op jit(solution)/shard_map/all_to_all | solution.py:23
  94.5 0.2 multiply_reduce_fusion
  94.8 12.4 %all-reduce = (f32[128]{0:T(128)S(1)}, f32[128]{0:T(128)S(1)}) all-reduce(f32[128]{0:T(128)S(1)} %get-tuple-element.22, f32[128]{0:T(128)S(1)} %fusion.10), channel_id=1, replica_groups=mesh['ctx'=128,'head'=8] {'head'}, use_global_device_ids=true, to_apply=%region_2.3 | all-reduce | flops 256 | bytes 2048 | tf_op jit(solution)/shard_map/psum | solution.py:57
  107.7 0.7 all_to_all.30
  108.4 6.7 %all-to-all-start.2 = ((f32[128,1,128]{2,1,0:T(1,128)}), f32[128,1,128]{2,1,0:T(1,128)S(1)}, u32[]{:S(2)}, u32[]{:S(2)}) async-start(f32[128,1,128]{2,1,0:T(1,128)} %bitcast.14), calls=%async_computation.2 | async-start | bytes 131072 | tf_op jit(solution)/shard_map/all_to_all | solution.py:16
  115.1 0.2 fusion.1
  115.4 26.3 %all-to-all-done.2 = f32[128,1,128]{2,1,0:T(1,128)S(1)} async-done(((f32[128,1,128]{2,1,0:T(1,128)}), f32[128,1,128]{2,1,0:T(1,128)S(1)}, u32[]{:S(2)}, u32[]{:S(2)}) %all-to-all-start.2) | async-done | bytes 65568 | tf_op jit(solution)/shard_map/all_to_all | solution.py:16
  141.8 0.6 rev.4
  142.5 6.4 %all-to-all-start.3 = ((f32[128,1,128]{2,1,0:T(1,128)}), f32[128,1,128]{2,1,0:T(1,128)S(1)}, u32[]{:S(2)}, u32[]{:S(2)}) async-start(f32[128,1,128]{2,1,0:T(1,128)} %bitcast.16), calls=%async_computation.3 | async-start | bytes 131072 | tf_op jit(solution)/shard_map/all_to_all | solution.py:23
  149.2 0.7 copy.57
  150.0 0.7 copy.56
  150.8 23.5 %all-to-all-done.3 = f32[128,1,128]{2,1,0:T(1,128)S(1)} async-done(((f32[128,1,128]{2,1,0:T(1,128)}), f32[128,1,128]{2,1,0:T(1,128)S(1)}, u32[]{:S(2)}, u32[]{:S(2)}) %all-to-all-start.3) | async-done | bytes 65568 | tf_op jit(solution)/shard_map/all_to_all | solution.py:23
  174.6 0.2 fusion.6
  174.8 0.7 copy.59
  175.7 0.8 copy.58
  (31 shorter events, 2.4 us)
Async XLA Ops:
  0.6 1.0 copy-start
  2.6 32.6 %copy-start.1 = (bf16[128,256]{1,0:T(8,128)(2,1)S(1)}, bf16[128,256]{1,0:T(8,128)(2,1)}, u32[]{:S(2)}) copy-start(bf16[128,256]{1,0:T(8,128)(2,1)} %param.5) | copy-start | bytes 196612
  2.6 59.1 %all-to-all-start = ((f32[128,1,128]{2,1,0:T(1,128)}), f32[128,1,128]{2,1,0:T(1,128)S(1)}, u32[]{:S(2)}, u32[]{:S(2)}) async-start(f32[128,1,128]{2,1,0:T(1,128)} %bitcast.4), calls=%async_computation | async-start | bytes 131072 | tf_op jit(solution)/shard_map/all_to_all | solution.py:16
  35.2 0.8 copy-start.2
  36.1 0.7 copy-start.3
  62.5 31.9 %all-to-all-start.1 = ((f32[128,1,128]{2,1,0:T(1,128)}), f32[128,1,128]{2,1,0:T(1,128)S(1)}, u32[]{:S(2)}, u32[]{:S(2)}) async-start(f32[128,1,128]{2,1,0:T(1,128)} %fusion.13), calls=%async_computation.1 | async-start | bytes 131072 | tf_op jit(solution)/shard_map/all_to_all | solution.py:23
  108.4 33.2 %all-to-all-start.2 = ((f32[128,1,128]{2,1,0:T(1,128)}), f32[128,1,128]{2,1,0:T(1,128)S(1)}, u32[]{:S(2)}, u32[]{:S(2)}) async-start(f32[128,1,128]{2,1,0:T(1,128)} %bitcast.14), calls=%async_computation.2 | async-start | bytes 131072 | tf_op jit(solution)/shard_map/all_to_all | solution.py:16
  142.5 31.9 %all-to-all-start.3 = ((f32[128,1,128]{2,1,0:T(1,128)}), f32[128,1,128]{2,1,0:T(1,128)S(1)}, u32[]{:S(2)}, u32[]{:S(2)}) async-start(f32[128,1,128]{2,1,0:T(1,128)} %bitcast.16), calls=%async_computation.3 | async-start | bytes 131072 | tf_op jit(solution)/shard_map/all_to_all | solution.py:23

commit v2 on v1

--- a/solution.py
+++ b/solution.py
@@ -14,14 +14,21 @@
     peers = lax.axis_size(axis)
     rows = value.reshape(peers, -1)
     mine = lax.all_to_all(rows, axis, 0, 0, tiled=True)
+    total = lax.cumsum(mine, axis=0, reverse=reverse)
+    zero = jnp.zeros_like(total[:1])
     if reverse:
-        mine = mine[::-1]
-    shifted = jnp.concatenate([jnp.zeros_like(mine[:1]), mine[:-1]], axis=0)
-    total = jnp.cumsum(shifted, axis=0)
-    if reverse:
-        total = total[::-1]
+        total = jnp.concatenate([total[1:], zero], axis=0)
+    else:
+        total = jnp.concatenate([zero, total[:-1]], axis=0)
     back = lax.all_to_all(total, axis, 0, 0, tiled=True)
     return lax.optimization_barrier(back).reshape(value.shape)
+
+
+def head_sum(value, axis):
+    peers = lax.axis_size(axis)
+    spread = jnp.broadcast_to(value[None], (peers,) + value.shape)
+    gathered = lax.all_to_all(spread, axis, 0, 0, tiled=True)
+    return jnp.sum(gathered, axis=0)
 
 
 def on_device(query_rows, key_rows, value_rows, norm_gain, cotangent):
@@ -54,10 +61,9 @@
     square_local = jnp.sum(flat * flat, axis=1)
     upstream = cotangent.astype(jnp.float32) * gain
     inner_local = jnp.sum(upstream * flat, axis=1)
-    square_all = lax.psum(square_local, "head")
+    square_all, inner_all = head_sum(jnp.stack([square_local, inner_local]), "head")
     recip = lax.rsqrt(square_all / width_all + EPS)
     normed = (flat * recip[:, None] * gain).astype(jnp.bfloat16)
-    inner_all = lax.psum(inner_local, "head")
     grad_flat = (
         recip[:, None] * upstream - flat * (recip * recip * recip * inner_all / width_all)[:, None]
     )

time: 177 us -> 175 us (0.989)
  the two profiles are of different devices: /device:TPU:32 before, /device:TPU:2 now
where the time goes in v2:
time: 175 us
  waiting for transfers between devices  101 us (58%)
  starting transfers between devices  51.8 us (30%)
  local copies, waits for them, and re-layouts  8.59 us (5%)
  blocking collectives  8.48 us (5%)
  matrix products  2.18 us (1%)
    all_to_all x2, waiting for transfers between devices, prefix(): mine = lax.all_to_all(rows, axis, 0, 0, tiled=True)  52.2 us
    all_to_all x2, waiting for transfers between devices, prefix(): back = lax.all_to_all(total, axis, 0, 0, tiled=True)  48.9 us
    all_to_all x2, starting transfers between devices, prefix(): mine = lax.all_to_all(rows, axis, 0, 0, tiled=True)  39.5 us
    all_to_all x2, starting transfers between devices, prefix(): back = lax.all_to_all(total, axis, 0, 0, tiled=True)  12.3 us
    all_to_all x1, blocking collectives, head_sum(): gathered = lax.all_to_all(spread, axis, 0, 0, tiled=True)  8.48 us
    unnamed x16, local copies, waits for them, and re-layouts  5.56 us
  transfers between devices with their start and end apart: 4, of which 4 were waited for; matrix products, arithmetic and copies ran while one was open for 2% of the time, Pallas kernels for 0%

profile of v2, /device:TPU:2, one launch (start us, length us, event | category | flops | bytes accessed | tf_op | source)
XLA Modules:
  0.0 174.6 jit_solution(1188707676694971976)
XLA Ops:
  0.6 1.0 copy.75
  1.9 0.7 all_to_all.35
  2.6 33.3 %all-to-all-start = ((f32[128,1,128]{2,1,0:T(1,128)}), f32[128,1,128]{2,1,0:T(1,128)S(1)}, u32[]{:S(2)}, u32[]{:S(2)}) async-start(f32[128,1,128]{2,1,0:T(1,128)} %bitcast.4), calls=%async_computation | async-start | bytes 131072 | tf_op jit(solution)/shard_map/all_to_all | solution.py:16
  36.1 0.7 copy-done.2
  37.0 0.5 copy-done.3
  37.5 25.3 %all-to-all-done = f32[128,1,128]{2,1,0:T(1,128)S(1)} async-done(((f32[128,1,128]{2,1,0:T(1,128)}), f32[128,1,128]{2,1,0:T(1,128)S(1)}, u32[]{:S(2)}, u32[]{:S(2)}) %all-to-all-start) | async-done | bytes 65568 | tf_op jit(solution)/shard_map/all_to_all | solution.py:16
  63.0 0.6 concatenate.6
  63.7 6.1 %all-to-all-start.1 = ((f32[128,1,128]{2,1,0:T(1,128)}), f32[128,1,128]{2,1,0:T(1,128)S(1)}, u32[]{:S(2)}, u32[]{:S(2)}) async-start(f32[128,1,128]{2,1,0:T(1,128)} %bitcast.7), calls=%async_computation.1 | async-start | bytes 131072 | tf_op jit(solution)/shard_map/all_to_all | solution.py:23
  69.8 0.2 fusion
  70.3 25.2 %all-to-all-done.1 = f32[128,1,128]{2,1,0:T(1,128)S(1)} async-done(((f32[128,1,128]{2,1,0:T(1,128)}), f32[128,1,128]{2,1,0:T(1,128)S(1)}, u32[]{:S(2)}, u32[]{:S(2)}) %all-to-all-start.1) | async-done | bytes 65568 | tf_op jit(solution)/shard_map/all_to_all | solution.py:23
  95.6 0.2 multiply_reduce_fusion
  96.0 8.5 %all_to_all.53 = f32[8,2,128]{2,1,0:T(2,128)S(1)} all-to-all(f32[8,2,128]{2,1,0:T(2,128)S(1)} %broadcast_in_dim.33), channel_id=1, replica_groups=mesh['ctx'=128,'head'=8] {'head'}, dimensions={0} | all-to-all | bytes 16384 | tf_op jit(solution)/shard_map/all_to_all | solution.py:30
  104.9 0.7 all_to_all.42
  105.6 6.1 %all-to-all-start.3 = ((f32[128,1,128]{2,1,0:T(1,128)}), f32[128,1,128]{2,1,0:T(1,128)S(1)}, u32[]{:S(2)}, u32[]{:S(2)}) async-start(f32[128,1,128]{2,1,0:T(1,128)} %bitcast.21), calls=%async_computation.3 | async-start | bytes 131072 | tf_op jit(solution)/shard_map/all_to_all | solution.py:16
  111.7 0.2 fusion.1
  112.0 26.9 %all-to-all-done.3 = f32[128,1,128]{2,1,0:T(1,128)S(1)} async-done(((f32[128,1,128]{2,1,0:T(1,128)}), f32[128,1,128]{2,1,0:T(1,128)S(1)}, u32[]{:S(2)}, u32[]{:S(2)}) %all-to-all-start.3) | async-done | bytes 65568 | tf_op jit(solution)/shard_map/all_to_all | solution.py:16
  138.8 1.1 reduce_window_sum.21
  140.0 0.6 concatenate.7
  140.6 6.1 %all-to-all-start.4 = ((f32[128,1,128]{2,1,0:T(1,128)}), f32[128,1,128]{2,1,0:T(1,128)S(1)}, u32[]{:S(2)}, u32[]{:S(2)}) async-start(f32[128,1,128]{2,1,0:T(1,128)} %bitcast.24), calls=%async_computation.4 | async-start | bytes 131072 | tf_op jit(solution)/shard_map/all_to_all | solution.py:23
  147.1 0.7 copy.87
  147.9 0.7 copy.86
  148.8 23.7 %all-to-all-done.4 = f32[128,1,128]{2,1,0:T(1,128)S(1)} async-done(((f32[128,1,128]{2,1,0:T(1,128)}), f32[128,1,128]{2,1,0:T(1,128)S(1)}, u32[]{:S(2)}, u32[]{:S(2)}) %all-to-all-start.4) | async-done | bytes 65568 | tf_op jit(solution)/shard_map/all_to_all | solution.py:23
  172.9 0.7 copy.89
  173.8 0.8 copy.88
  (34 shorter events, 2.6 us)
Async XLA Ops:
  0.6 1.0 copy-start
  2.6 33.3 %copy-start.1 = (bf16[128,256]{1,0:T(8,128)(2,1)S(1)}, bf16[128,256]{1,0:T(8,128)(2,1)}, u32[]{:S(2)}) copy-start(bf16[128,256]{1,0:T(8,128)(2,1)} %param.5) | copy-start | bytes 196612
  2.6 60.2 %all-to-all-start = ((f32[128,1,128]{2,1,0:T(1,128)}), f32[128,1,128]{2,1,0:T(1,128)S(1)}, u32[]{:S(2)}, u32[]{:S(2)}) async-start(f32[128,1,128]{2,1,0:T(1,128)} %bitcast.4), calls=%async_computation | async-start | bytes 131072 | tf_op jit(solution)/shard_map/all_to_all | solution.py:16
  36.0 0.8 copy-start.2
  36.8 0.7 copy-start.3
  63.7 31.8 %all-to-all-start.1 = ((f32[128,1,128]{2,1,0:T(1,128)}), f32[128,1,128]{2,1,0:T(1,128)S(1)}, u32[]{:S(2)}, u32[]{:S(2)}) async-start(f32[128,1,128]{2,1,0:T(1,128)} %bitcast.7), calls=%async_computation.1 | async-start | bytes 131072 | tf_op jit(solution)/shard_map/all_to_all | solution.py:23
  105.6 33.3 %all-to-all-start.3 = ((f32[128,1,128]{2,1,0:T(1,128)}), f32[128,1,128]{2,1,0:T(1,128)S(1)}, u32[]{:S(2)}, u32[]{:S(2)}) async-start(f32[128,1,128]{2,1,0:T(1,128)} %bitcast.21), calls=%async_computation.3 | async-start | bytes 131072 | tf_op jit(solution)/shard_map/all_to_all | solution.py:16
  140.6 31.8 %all-to-all-start.4 = ((f32[128,1,128]{2,1,0:T(1,128)}), f32[128,1,128]{2,1,0:T(1,128)S(1)}, u32[]{:S(2)}, u32[]{:S(2)}) async-start(f32[128,1,128]{2,1,0:T(1,128)} %bitcast.24), calls=%async_computation.4 | async-start | bytes 131072 | tf_op jit(solution)/shard_map/all_to_all | solution.py:23

commit v3 on v2

--- a/solution.py
+++ b/solution.py
@@ -14,12 +14,10 @@
     peers = lax.axis_size(axis)
     rows = value.reshape(peers, -1)
     mine = lax.all_to_all(rows, axis, 0, 0, tiled=True)
-    total = lax.cumsum(mine, axis=0, reverse=reverse)
-    zero = jnp.zeros_like(total[:1])
-    if reverse:
-        total = jnp.concatenate([total[1:], zero], axis=0)
-    else:
-        total = jnp.concatenate([zero, total[:-1]], axis=0)
+    row = lax.broadcasted_iota(jnp.int32, (peers, peers), 0)
+    col = lax.broadcasted_iota(jnp.int32, (peers, peers), 1)
+    before = (col > row) if reverse else (col < row)
+    total = jnp.dot(before.astype(mine.dtype), mine, precision=lax.Precision.HIGHEST)
     back = lax.all_to_all(total, axis, 0, 0, tiled=True)
     return lax.optimization_barrier(back).reshape(value.shape)
 

time: 175 us -> 174 us (level)
  no operation moved by 1% of the time
where the time goes in v3:
time: 174 us
  waiting for transfers between devices  101 us (58%)
  starting transfers between devices  51.8 us (30%)
  blocking collectives  8.48 us (5%)
  local copies, waits for them, and re-layouts  7.3 us (4%)
  matrix products  3.8 us (2%)
    all_to_all x2, waiting for transfers between devices, prefix(): mine = lax.all_to_all(rows, axis, 0, 0, tiled=True)  52.2 us
    all_to_all x2, waiting for transfers between devices, prefix(): back = lax.all_to_all(total, axis, 0, 0, tiled=True)  48.9 us
    all_to_all x2, starting transfers between devices, prefix(): mine = lax.all_to_all(rows, axis, 0, 0, tiled=True)  39.5 us
    all_to_all x2, starting transfers between devices, prefix(): back = lax.all_to_all(total, axis, 0, 0, tiled=True)  12.3 us
    all_to_all x1, blocking collectives, head_sum(): gathered = lax.all_to_all(spread, axis, 0, 0, tiled=True)  8.48 us
    unnamed x16, local copies, waits for them, and re-layouts  5.56 us
  transfers between devices with their start and end apart: 4, of which 4 were waited for; matrix products, arithmetic and copies ran while one was open for 2% of the time, Pallas kernels for 0%

profile of v3, /device:TPU:2, one launch (start us, length us, event | category | flops | bytes accessed | tf_op | source)
XLA Modules:
  0.0 173.6 jit_solution(13085328344154187633)
XLA Ops:
  0.6 1.0 copy.75
  1.9 0.7 all_to_all.35
  2.6 33.3 %all-to-all-start = ((f32[128,1,128]{2,1,0:T(1,128)}), f32[128,1,128]{2,1,0:T(1,128)S(1)}, u32[]{:S(2)}, u32[]{:S(2)}) async-start(f32[128,1,128]{2,1,0:T(1,128)} %bitcast.4), calls=%async_computation | async-start | bytes 131072 | tf_op jit(solution)/shard_map/all_to_all | solution.py:16
  36.1 0.7 copy-done.2
  37.0 0.5 copy-done.3
  37.5 25.3 %all-to-all-done = f32[128,1,128]{2,1,0:T(1,128)S(1)} async-done(((f32[128,1,128]{2,1,0:T(1,128)}), f32[128,1,128]{2,1,0:T(1,128)S(1)}, u32[]{:S(2)}, u32[]{:S(2)}) %all-to-all-start) | async-done | bytes 65568 | tf_op jit(solution)/shard_map/all_to_all | solution.py:16
  62.8 0.8 fusion.13
  63.7 6.1 %all-to-all-start.1 = ((f32[128,1,128]{2,1,0:T(1,128)}), f32[128,1,128]{2,1,0:T(1,128)S(1)}, u32[]{:S(2)}, u32[]{:S(2)}) async-start(f32[128,1,128]{2,1,0:T(1,128)} %bitcast.7), calls=%async_computation.1 | async-start | bytes 131072 | tf_op jit(solution)/shard_map/all_to_all | solution.py:21
  69.8 0.2 fusion
  70.3 25.2 %all-to-all-done.1 = f32[128,1,128]{2,1,0:T(1,128)S(1)} async-done(((f32[128,1,128]{2,1,0:T(1,128)}), f32[128,1,128]{2,1,0:T(1,128)S(1)}, u32[]{:S(2)}, u32[]{:S(2)}) %all-to-all-start.1) | async-done | bytes 65568 | tf_op jit(solution)/shard_map/all_to_all | solution.py:21
  95.6 0.2 multiply_reduce_fusion
  95.9 8.5 %all_to_all.53 = f32[8,2,128]{2,1,0:T(2,128)S(1)} all-to-all(f32[8,2,128]{2,1,0:T(2,128)S(1)} %broadcast_in_dim.33), channel_id=1, replica_groups=mesh['ctx'=128,'head'=8] {'head'}, dimensions={0} | all-to-all | bytes 16384 | tf_op jit(solution)/shard_map/all_to_all | solution.py:28
  104.9 0.7 all_to_all.42
  105.6 6.1 %all-to-all-start.3 = ((f32[128,1,128]{2,1,0:T(1,128)}), f32[128,1,128]{2,1,0:T(1,128)S(1)}, u32[]{:S(2)}, u32[]{:S(2)}) async-start(f32[128,1,128]{2,1,0:T(1,128)} %bitcast.21), calls=%async_computation.3 | async-start | bytes 131072 | tf_op jit(solution)/shard_map/all_to_all | solution.py:16
  111.7 0.2 fusion.1
  112.0 26.9 %all-to-all-done.3 = f32[128,1,128]{2,1,0:T(1,128)S(1)} async-done(((f32[128,1,128]{2,1,0:T(1,128)}), f32[128,1,128]{2,1,0:T(1,128)S(1)}, u32[]{:S(2)}, u32[]{:S(2)}) %all-to-all-start.3) | async-done | bytes 65568 | tf_op jit(solution)/shard_map/all_to_all | solution.py:16
  138.8 0.8 fusion.14
  139.7 6.1 %all-to-all-start.4 = ((f32[128,1,128]{2,1,0:T(1,128)}), f32[128,1,128]{2,1,0:T(1,128)S(1)}, u32[]{:S(2)}, u32[]{:S(2)}) async-start(f32[128,1,128]{2,1,0:T(1,128)} %bitcast.24), calls=%async_computation.4 | async-start | bytes 131072 | tf_op jit(solution)/shard_map/all_to_all | solution.py:21
  146.2 0.7 copy.87
  146.9 0.7 copy.86
  147.8 23.7 %all-to-all-done.4 = f32[128,1,128]{2,1,0:T(1,128)S(1)} async-done(((f32[128,1,128]{2,1,0:T(1,128)}), f32[128,1,128]{2,1,0:T(1,128)S(1)}, u32[]{:S(2)}, u32[]{:S(2)}) %all-to-all-start.4) | async-done | bytes 65568 | tf_op jit(solution)/shard_map/all_to_all | solution.py:21
  171.7 0.2 fusion.6
  171.9 0.7 copy.89
  172.8 0.8 copy.88
  (31 shorter events, 2.2 us)
Async XLA Ops:
  0.6 1.0 copy-start
  2.6 33.3 %copy-start.1 = (bf16[128,256]{1,0:T(8,128)(2,1)S(1)}, bf16[128,256]{1,0:T(8,128)(2,1)}, u32[]{:S(2)}) copy-start(bf16[128,256]{1,0:T(8,128)(2,1)} %param.5) | copy-start | bytes 196612
  2.6 60.2 %all-to-all-start = ((f32[128,1,128]{2,1,0:T(1,128)}), f32[128,1,128]{2,1,0:T(1,128)S(1)}, u32[]{:S(2)}, u32[]{:S(2)}) async-start(f32[128,1,128]{2,1,0:T(1,128)} %bitcast.4), calls=%async_computation | async-start | bytes 131072 | tf_op jit(solution)/shard_map/all_to_all | solution.py:16
  36.0 0.8 copy-start.2
  36.8 0.7 copy-start.3
  63.7 31.8 %all-to-all-start.1 = ((f32[128,1,128]{2,1,0:T(1,128)}), f32[128,1,128]{2,1,0:T(1,128)S(1)}, u32[]{:S(2)}, u32[]{:S(2)}) async-start(f32[128,1,128]{2,1,0:T(1,128)} %bitcast.7), calls=%async_computation.1 | async-start | bytes 131072 | tf_op jit(solution)/shard_map/all_to_all | solution.py:21
  105.6 33.3 %all-to-all-start.3 = ((f32[128,1,128]{2,1,0:T(1,128)}), f32[128,1,128]{2,1,0:T(1,128)S(1)}, u32[]{:S(2)}, u32[]{:S(2)}) async-start(f32[128,1,128]{2,1,0:T(1,128)} %bitcast.21), calls=%async_computation.3 | async-start | bytes 131072 | tf_op jit(solution)/shard_map/all_to_all | solution.py:16
  139.7 31.8 %all-to-all-start.4 = ((f32[128,1,128]{2,1,0:T(1,128)}), f32[128,1,128]{2,1,0:T(1,128)S(1)}, u32[]{:S(2)}, u32[]{:S(2)}) async-start(f32[128,1,128]{2,1,0:T(1,128)} %bitcast.24), calls=%async_computation.4 | async-start | bytes 131072 | tf_op jit(solution)/shard_map/all_to_all | solution.py:21

commit v4 on v3

--- a/solution.py
+++ b/solution.py
@@ -44,8 +44,11 @@
     causal = lax.broadcasted_iota(jnp.int32, (tokens_here, tokens_here), 0) >= lax.broadcasted_iota(
         jnp.int32, (tokens_here, tokens_here), 1
     )
-    local_state = jnp.einsum(
-        "thd,the->hde", key_local, value_local, preferred_element_type=jnp.float32
+    every_pair = lax.dot_general(
+        key_rows, value_rows, (((0,), (0,)), ((), ())), preferred_element_type=jnp.float32
+    )
+    local_state = jnp.stack(
+        [every_pair[h * HEAD_DIM:(h + 1) * HEAD_DIM, h * HEAD_DIM:(h + 1) * HEAD_DIM] for h in range(heads_here)]
     )
     carried = prefix(local_state, "ctx", False)
     carried_bf = carried.astype(jnp.bfloat16)
@@ -79,13 +82,21 @@
     local_grad = jnp.einsum("thd,the->hde", queries, grad_out, preferred_element_type=jnp.float32)
     later = prefix(local_grad, "ctx", True)
     later_bf = later.astype(jnp.bfloat16)
+    width_here = heads_here * HEAD_DIM
+    same_head = (
+        lax.broadcasted_iota(jnp.int32, (width_here, width_here), 0) // HEAD_DIM
+        == lax.broadcasted_iota(jnp.int32, (width_here, width_here), 1) // HEAD_DIM
+    )
+    tiled = jnp.tile(later_bf.reshape(width_here, HEAD_DIM), (1, heads_here))
+    by_value = jnp.where(same_head, tiled, jnp.zeros_like(tiled))
+    by_key = jnp.where(same_head, tiled.T, jnp.zeros_like(tiled))
     key_grad = jnp.einsum("hts,thd->shd", grad_masked, queries, preferred_element_type=jnp.float32)
-    key_grad = key_grad + jnp.einsum(
-        "she,hde->shd", value_local, later_bf, preferred_element_type=jnp.float32
+    key_grad = key_grad.reshape(tokens_here, width_here) + jnp.dot(
+        value_rows, by_key, preferred_element_type=jnp.float32
     )
     value_grad = jnp.einsum("hts,thd->shd", masked, grad_out, preferred_element_type=jnp.float32)
-    value_grad = value_grad + jnp.einsum(
-        "shd,hde->she", key_local, later_bf, preferred_element_type=jnp.float32
+    value_grad = value_grad.reshape(tokens_here, width_here) + jnp.dot(
+        key_rows, by_value, preferred_element_type=jnp.float32
     )
     shape = (tokens_here, heads_here * HEAD_DIM)
     return (

time: 174 us -> 175 us (level)
  blocking collectives: 8.48 us -> 0 us
  starting transfers between devices: 51.8 us -> 56.6 us
  waiting for transfers between devices: 101 us -> 103 us
    all_to_all x1 -> x0, blocking collectives: 8.48 us -> none  [head_sum(): gathered = lax.all_to_all(spread, axis, 0, 0, tiled=True)]
    all_to_all x0 -> x1, starting transfers between devices: none -> 4.83 us  [head_sum(): gathered = lax.all_to_all(spread, axis, 0, 0, tiled=True)]
    all_to_all x0 -> x1, waiting for transfers between devices: none -> 3.85 us  [head_sum(): gathered = lax.all_to_all(spread, axis, 0, 0, tiled=True)]
    all_to_all x2, waiting for transfers between devices: 52.2 us -> 50.3 us  [prefix(): mine = lax.all_to_all(rows, axis, 0, 0, tiled=True)]
    unnamed x16 -> x18, local copies, waits for them, and re-layouts: 5.56 us -> 6.12 us
  transfers between devices with their start and end apart: 4 -> 5, of which waited for: 4 -> 5; matrix products, arithmetic and copies ran while one was open for 2% -> 2% of each run, Pallas kernels for 0% -> 0%
where the time goes in v4:
time: 175 us
  waiting for transfers between devices  103 us (59%)
  starting transfers between devices  56.6 us (32%)
  local copies, waits for them, and re-layouts  8.73 us (5%)
  matrix products  5.11 us (3%)
    all_to_all x2, waiting for transfers between devices, prefix(): mine = lax.all_to_all(rows, axis, 0, 0, tiled=True)  50.3 us
    all_to_all x2, waiting for transfers between devices, prefix(): back = lax.all_to_all(total, axis, 0, 0, tiled=True)  48.9 us
    all_to_all x2, starting transfers between devices, prefix(): mine = lax.all_to_all(rows, axis, 0, 0, tiled=True)  39.5 us
    all_to_all x2, starting transfers between devices, prefix(): back = lax.all_to_all(total, axis, 0, 0, tiled=True)  12.3 us
    unnamed x18, local copies, waits for them, and re-layouts  6.12 us
    all_to_all x1, starting transfers between devices, head_sum(): gathered = lax.all_to_all(spread, axis, 0, 0, tiled=True)  4.83 us
    all_to_all x1, waiting for transfers between devices, head_sum(): gathered = lax.all_to_all(spread, axis, 0, 0, tiled=True)  3.85 us
  transfers between devices with their start and end apart: 5, of which 5 were waited for; matrix products, arithmetic and copies ran while one was open for 2% of the time, Pallas kernels for 0%

profile of v4, /device:TPU:2, one launch (start us, length us, event | category | flops | bytes accessed | tf_op | source)
XLA Modules:
  0.0 174.7 jit_solution(3504431225538366427)
XLA Ops:
  0.6 1.1 fusion.38
  1.8 0.7 all_to_all.35
  2.5 33.3 %all-to-all-start = ((f32[128,1,128]{2,1,0:T(1,128)}), f32[128,1,128]{2,1,0:T(1,128)S(1)}, u32[]{:S(2)}, u32[]{:S(2)}) async-start(f32[128,1,128]{2,1,0:T(1,128)} %bitcast.8), calls=%async_computation | async-start | bytes 131072 | tf_op jit(solution)/shard_map/all_to_all | solution.py:16
  36.0 0.7 copy-done
  36.8 0.7 copy-done.2
  37.7 0.7 copy-done.3
  38.5 0.5 copy-done.4
  39.1 23.7 %all-to-all-done = f32[128,1,128]{2,1,0:T(1,128)S(1)} async-done(((f32[128,1,128]{2,1,0:T(1,128)}), f32[128,1,128]{2,1,0:T(1,128)S(1)}, u32[]{:S(2)}, u32[]{:S(2)}) %all-to-all-start) | async-done | bytes 65568 | tf_op jit(solution)/shard_map/all_to_all | solution.py:16
  62.7 0.8 fusion.32
  63.5 6.1 %all-to-all-start.1 = ((f32[128,1,128]{2,1,0:T(1,128)}), f32[128,1,128]{2,1,0:T(1,128)S(1)}, u32[]{:S(2)}, u32[]{:S(2)}) async-start(f32[128,1,128]{2,1,0:T(1,128)} %bitcast.11), calls=%async_computation.1 | async-start | bytes 131072 | tf_op jit(solution)/shard_map/all_to_all | solution.py:21
  70.1 25.2 %all-to-all-done.1 = f32[128,1,128]{2,1,0:T(1,128)S(1)} async-done(((f32[128,1,128]{2,1,0:T(1,128)}), f32[128,1,128]{2,1,0:T(1,128)S(1)}, u32[]{:S(2)}, u32[]{:S(2)}) %all-to-all-start.1) | async-done | bytes 65568 | tf_op jit(solution)/shard_map/all_to_all | solution.py:21
  95.8 0.6 broadcast_in_dim.33
  96.4 4.8 %all-to-all-start.2 = ((f32[8,2,128]{2,1,0:T(2,128)}), f32[8,2,128]{2,1,0:T(2,128)S(1)}, u32[]{:S(2)}, u32[]{:S(2)}) async-start(f32[8,2,128]{2,1,0:T(2,128)} %broadcast_in_dim.33), calls=%async_computation.2 | async-start | bytes 16384 | tf_op jit(solution)/shard_map/all_to_all | solution.py:28
  101.3 3.8 %all-to-all-done.2 = f32[8,2,128]{2,1,0:T(2,128)S(1)} async-done(((f32[8,2,128]{2,1,0:T(2,128)}), f32[8,2,128]{2,1,0:T(2,128)S(1)}, u32[]{:S(2)}, u32[]{:S(2)}) %all-to-all-start.2) | async-done | bytes 8224 | tf_op jit(solution)/shard_map/all_to_all | solution.py:28
  105.6 0.7 all_to_all.42
  106.3 6.1 %all-to-all-start.3 = ((f32[128,1,128]{2,1,0:T(1,128)}), f32[128,1,128]{2,1,0:T(1,128)S(1)}, u32[]{:S(2)}, u32[]{:S(2)}) async-start(f32[128,1,128]{2,1,0:T(1,128)} %bitcast.26), calls=%async_computation.3 | async-start | bytes 131072 | tf_op jit(solution)/shard_map/all_to_all | solution.py:16
  112.9 26.7 %all-to-all-done.3 = f32[128,1,128]{2,1,0:T(1,128)S(1)} async-done(((f32[128,1,128]{2,1,0:T(1,128)}), f32[128,1,128]{2,1,0:T(1,128)S(1)}, u32[]{:S(2)}, u32[]{:S(2)}) %all-to-all-start.3) | async-done | bytes 65568 | tf_op jit(solution)/shard_map/all_to_all | solution.py:16
  139.5 0.8 fusion.33
  140.3 6.1 %all-to-all-start.4 = ((f32[128,1,128]{2,1,0:T(1,128)}), f32[128,1,128]{2,1,0:T(1,128)S(1)}, u32[]{:S(2)}, u32[]{:S(2)}) async-start(f32[128,1,128]{2,1,0:T(1,128)} %bitcast.29), calls=%async_computation.4 | async-start | bytes 131072 | tf_op jit(solution)/shard_map/all_to_all | solution.py:21
  146.6 0.7 copy.87
  147.4 0.7 copy.88
  148.4 23.7 %all-to-all-done.4 = f32[128,1,128]{2,1,0:T(1,128)S(1)} async-done(((f32[128,1,128]{2,1,0:T(1,128)}), f32[128,1,128]{2,1,0:T(1,128)S(1)}, u32[]{:S(2)}, u32[]{:S(2)}) %all-to-all-start.4) | async-done | bytes 65568 | tf_op jit(solution)/shard_map/all_to_all | solution.py:21
  172.8 0.7 copy.89
  174.0 0.7 copy.90
  (41 shorter events, 3.8 us)
Async XLA Ops:
  2.5 33.3 %copy-start.1 = (bf16[128,256]{1,0:T(8,128)(2,1)S(1)}, bf16[128,256]{1,0:T(8,128)(2,1)}, u32[]{:S(2)}) copy-start(bf16[128,256]{1,0:T(8,128)(2,1)} %param.6) | copy-start | bytes 196612
  2.5 60.2 %all-to-all-start = ((f32[128,1,128]{2,1,0:T(1,128)}), f32[128,1,128]{2,1,0:T(1,128)S(1)}, u32[]{:S(2)}, u32[]{:S(2)}) async-start(f32[128,1,128]{2,1,0:T(1,128)} %bitcast.8), calls=%async_computation | async-start | bytes 131072 | tf_op jit(solution)/shard_map/all_to_all | solution.py:16
  35.9 0.8 copy-start
  36.7 0.8 copy-start.2
  37.6 0.8 copy-start.3
  38.4 0.7 copy-start.4
  63.5 31.8 %all-to-all-start.1 = ((f32[128,1,128]{2,1,0:T(1,128)}), f32[128,1,128]{2,1,0:T(1,128)S(1)}, u32[]{:S(2)}, u32[]{:S(2)}) async-start(f32[128,1,128]{2,1,0:T(1,128)} %bitcast.11), calls=%async_computation.1 | async-start | bytes 131072 | tf_op jit(solution)/shard_map/all_to_all | solution.py:21
  96.4 8.7 %all-to-all-start.2 = ((f32[8,2,128]{2,1,0:T(2,128)}), f32[8,2,128]{2,1,0:T(2,128)S(1)}, u32[]{:S(2)}, u32[]{:S(2)}) async-start(f32[8,2,128]{2,1,0:T(2,128)} %broadcast_in_dim.33), calls=%async_computation.2 | async-start | bytes 16384 | tf_op jit(solution)/shard_map/all_to_all | solution.py:28
  106.3 33.3 %all-to-all-start.3 = ((f32[128,1,128]{2,1,0:T(1,128)}), f32[128,1,128]{2,1,0:T(1,128)S(1)}, u32[]{:S(2)}, u32[]{:S(2)}) async-start(f32[128,1,128]{2,1,0:T(1,128)} %bitcast.26), calls=%async_computation.3 | async-start | bytes 131072 | tf_op jit(solution)/shard_map/all_to_all | solution.py:16
  140.3 31.8 %all-to-all-start.4 = ((f32[128,1,128]{2,1,0:T(1,128)}), f32[128,1,128]{2,1,0:T(1,128)S(1)}, u32[]{:S(2)}, u32[]{:S(2)}) async-start(f32[128,1,128]{2,1,0:T(1,128)} %bitcast.29), calls=%async_computation.4 | async-start | bytes 131072 | tf_op jit(solution)/shard_map/all_to_all | solution.py:21

commit v5 on v3

--- a/solution.py
+++ b/solution.py
@@ -1,7 +1,7 @@
 import jax
 import jax.numpy as jnp
 from jax import lax
-from jax.sharding import PartitionSpec as P
+from jax.sharding import Mesh, PartitionSpec as P
 
 HEADS = 32
 HEAD_DIM = 64
@@ -10,15 +10,18 @@
 EPS = 1e-05
 
 
-def prefix(value, axis, reverse):
-    peers = lax.axis_size(axis)
+def prefix(value, axes, reverse):
+    rows_axis, cols_axis = axes
+    rows_n, cols_n = lax.axis_size(rows_axis), lax.axis_size(cols_axis)
+    peers = rows_n * cols_n
     rows = value.reshape(peers, -1)
-    mine = lax.all_to_all(rows, axis, 0, 0, tiled=True)
-    row = lax.broadcasted_iota(jnp.int32, (peers, peers), 0)
-    col = lax.broadcasted_iota(jnp.int32, (peers, peers), 1)
+    mine = lax.all_to_all(rows, (cols_axis, rows_axis), 0, 0, tiled=True)
+    slot = lax.broadcasted_iota(jnp.int32, (peers,), 0)
+    order = (slot % rows_n) * cols_n + slot // rows_n
+    row, col = order[:, None], order[None, :]
     before = (col > row) if reverse else (col < row)
     total = jnp.dot(before.astype(mine.dtype), mine, precision=lax.Precision.HIGHEST)
-    back = lax.all_to_all(total, axis, 0, 0, tiled=True)
+    back = lax.all_to_all(total, (cols_axis, rows_axis), 0, 0, tiled=True)
     return lax.optimization_barrier(back).reshape(value.shape)
 
 
@@ -47,7 +50,7 @@
     local_state = jnp.einsum(
         "thd,the->hde", key_local, value_local, preferred_element_type=jnp.float32
     )
-    carried = prefix(local_state, "ctx", False)
+    carried = prefix(local_state, ("ctx_rows", "ctx_cols"), False)
     carried_bf = carried.astype(jnp.bfloat16)
     scores = jnp.einsum("thd,shd->hts", queries, key_local, preferred_element_type=jnp.float32)
     masked = jnp.where(causal[None], scores, 0.0).astype(jnp.bfloat16)
@@ -77,7 +80,7 @@
         "the,hde->thd", grad_out, carried_bf, preferred_element_type=jnp.float32
     )
     local_grad = jnp.einsum("thd,the->hde", queries, grad_out, preferred_element_type=jnp.float32)
-    later = prefix(local_grad, "ctx", True)
+    later = prefix(local_grad, ("ctx_rows", "ctx_cols"), True)
     later_bf = later.astype(jnp.bfloat16)
     key_grad = jnp.einsum("hts,thd->shd", grad_masked, queries, preferred_element_type=jnp.float32)
     key_grad = key_grad + jnp.einsum(
@@ -96,12 +99,22 @@
     )
 
 
+def ctx_split(mesh):
+    ctx_devices = mesh.devices[:, 0]
+    rows_n = len({device.coords[1] for device in ctx_devices})
+    return rows_n, len(ctx_devices) // rows_n
+
+
 def solution(mesh):
-    placed = (P("ctx", "head"), P("ctx", "head"), P("ctx", "head"), P("head"), P("ctx", "head"))
+    rows_n, cols_n = ctx_split(mesh)
+    heads_n = mesh.devices.shape[1]
+    split = Mesh(mesh.devices.reshape(rows_n, cols_n, heads_n), ("ctx_rows", "ctx_cols", "head"))
+    rows = P(("ctx_rows", "ctx_cols"), "head")
+    placed = (rows, rows, rows, P("head"), rows)
     return jax.shard_map(
         on_device,
-        mesh=mesh,
+        mesh=split,
         in_specs=placed,
-        out_specs=(P("ctx", "head"), P("ctx", "head"), P("ctx", "head"), P("ctx", "head")),
+        out_specs=(rows, rows, rows, rows),
         check_vma=False,
     )

time: 174 us -> 171 us (0.983)
  the two profiles are of different devices: /device:TPU:2 before, /device:TPU:32 now
where the time goes in v5:
time: 171 us
  waiting for transfers between devices  98.1 us (57%)
  starting transfers between devices  50.7 us (30%)
  blocking collectives  9.41 us (6%)
  local copies, waits for them, and re-layouts  7.3 us (4%)
  matrix products  3.9 us (2%)
    all_to_all x2, waiting for transfers between devices, prefix(): mine = lax.all_to_all(rows, (cols_axis, rows_axis), 0, 0, tiled=True)  50 us
    all_to_all x2, waiting for transfers between devices, prefix(): back = lax.all_to_all(total, (cols_axis, rows_axis), 0, 0, tiled=True)  48 us
    all_to_all x2, starting transfers between devices, prefix(): mine = lax.all_to_all(rows, (cols_axis, rows_axis), 0, 0, tiled=True)  38.6 us
    all_to_all x2, starting transfers between devices, prefix(): back = lax.all_to_all(total, (cols_axis, rows_axis), 0, 0, tiled=True)  12.1 us
    all_to_all x1, blocking collectives, head_sum(): gathered = lax.all_to_all(spread, axis, 0, 0, tiled=True)  9.41 us
    unnamed x16, local copies, waits for them, and re-layouts  5.56 us
  transfers between devices with their start and end apart: 4, of which 4 were waited for; matrix products, arithmetic and copies ran while one was open for 2% of the time, Pallas kernels for 0%

profile of v5, /device:TPU:32, one launch (start us, length us, event | category | flops | bytes accessed | tf_op | source)
XLA Modules:
  0.0 170.5 jit_solution(2669265505978130766)
XLA Ops:
  0.6 1.0 copy.75
  1.9 0.7 all_to_all.35
  2.6 32.6 %all-to-all-start = ((f32[128,1,128]{2,1,0:T(1,128)}), f32[128,1,128]{2,1,0:T(1,128)S(1)}, u32[]{:S(2)}, u32[]{:S(2)}) async-start(f32[128,1,128]{2,1,0:T(1,128)} %bitcast.4), calls=%async_computation | async-start | bytes 131072 | tf_op jit(solution)/shard_map/all_to_all | solution.py:18
  35.3 0.7 copy-done.2
  36.2 0.5 copy-done.3
  36.7 24.4 %all-to-all-done = f32[128,1,128]{2,1,0:T(1,128)S(1)} async-done(((f32[128,1,128]{2,1,0:T(1,128)}), f32[128,1,128]{2,1,0:T(1,128)S(1)}, u32[]{:S(2)}, u32[]{:S(2)}) %all-to-all-start) | async-done | bytes 65568 | tf_op jit(solution)/shard_map/all_to_all | solution.py:18
  61.1 0.9 fusion.15
  62.0 6.0 %all-to-all-start.1 = ((f32[128,1,128]{2,1,0:T(1,128)}), f32[128,1,128]{2,1,0:T(1,128)S(1)}, u32[]{:S(2)}, u32[]{:S(2)}) async-start(f32[128,1,128]{2,1,0:T(1,128)} %bitcast.7), calls=%async_computation.1 | async-start | bytes 131072 | tf_op jit(solution)/shard_map/all_to_all | solution.py:24
  68.0 0.2 fusion
  68.4 24.8 %all-to-all-done.1 = f32[128,1,128]{2,1,0:T(1,128)S(1)} async-done(((f32[128,1,128]{2,1,0:T(1,128)}), f32[128,1,128]{2,1,0:T(1,128)S(1)}, u32[]{:S(2)}, u32[]{:S(2)}) %all-to-all-start.1) | async-done | bytes 65568 | tf_op jit(solution)/shard_map/all_to_all | solution.py:24
  93.3 0.2 multiply_reduce_fusion
  93.7 9.4 %all_to_all.53 = f32[8,2,128]{2,1,0:T(2,128)S(1)} all-to-all(f32[8,2,128]{2,1,0:T(2,128)S(1)} %broadcast_in_dim.22), channel_id=1, replica_groups=mesh['ctx_rows'=4,'ctx_cols'=32,'head'=8] {'head'}, dimensions={0} | all-to-all | bytes 16384 | tf_op jit(solution)/shard_map/all_to_all | solution.py:31
  103.6 0.7 all_to_all.42
  104.3 6.1 %all-to-all-start.3 = ((f32[128,1,128]{2,1,0:T(1,128)}), f32[128,1,128]{2,1,0:T(1,128)S(1)}, u32[]{:S(2)}, u32[]{:S(2)}) async-start(f32[128,1,128]{2,1,0:T(1,128)} %bitcast.21), calls=%async_computation.3 | async-start | bytes 131072 | tf_op jit(solution)/shard_map/all_to_all | solution.py:18
  110.4 0.2 fusion.1
  110.6 25.7 %all-to-all-done.3 = f32[128,1,128]{2,1,0:T(1,128)S(1)} async-done(((f32[128,1,128]{2,1,0:T(1,128)}), f32[128,1,128]{2,1,0:T(1,128)S(1)}, u32[]{:S(2)}, u32[]{:S(2)}) %all-to-all-start.3) | async-done | bytes 65568 | tf_op jit(solution)/shard_map/all_to_all | solution.py:18
  136.3 0.9 fusion.13
  137.1 6.0 %all-to-all-start.4 = ((f32[128,1,128]{2,1,0:T(1,128)}), f32[128,1,128]{2,1,0:T(1,128)S(1)}, u32[]{:S(2)}, u32[]{:S(2)}) async-start(f32[128,1,128]{2,1,0:T(1,128)} %bitcast.24), calls=%async_computation.4 | async-start | bytes 131072 | tf_op jit(solution)/shard_map/all_to_all | solution.py:24
  143.5 0.7 copy.87
  144.2 0.7 copy.86
  145.1 23.3 %all-to-all-done.4 = f32[128,1,128]{2,1,0:T(1,128)S(1)} async-done(((f32[128,1,128]{2,1,0:T(1,128)}), f32[128,1,128]{2,1,0:T(1,128)S(1)}, u32[]{:S(2)}, u32[]{:S(2)}) %all-to-all-start.4) | async-done | bytes 65568 | tf_op jit(solution)/shard_map/all_to_all | solution.py:24
  168.6 0.2 fusion.6
  168.9 0.7 copy.89
  169.8 0.8 copy.88
  (32 shorter events, 2.2 us)
Async XLA Ops:
  0.6 1.0 copy-start
  2.6 32.6 %copy-start.1 = (bf16[128,256]{1,0:T(8,128)(2,1)S(1)}, bf16[128,256]{1,0:T(8,128)(2,1)}, u32[]{:S(2)}) copy-start(bf16[128,256]{1,0:T(8,128)(2,1)} %param.5) | copy-start | bytes 196612
  2.6 58.5 %all-to-all-start = ((f32[128,1,128]{2,1,0:T(1,128)}), f32[128,1,128]{2,1,0:T(1,128)S(1)}, u32[]{:S(2)}, u32[]{:S(2)}) async-start(f32[128,1,128]{2,1,0:T(1,128)} %bitcast.4), calls=%async_computation | async-start | bytes 131072 | tf_op jit(solution)/shard_map/all_to_all | solution.py:18
  35.2 0.8 copy-start.2
  36.1 0.7 copy-start.3
  62.0 31.3 %all-to-all-start.1 = ((f32[128,1,128]{2,1,0:T(1,128)}), f32[128,1,128]{2,1,0:T(1,128)S(1)}, u32[]{:S(2)}, u32[]{:S(2)}) async-start(f32[128,1,128]{2,1,0:T(1,128)} %bitcast.7), calls=%async_computation.1 | async-start | bytes 131072 | tf_op jit(solution)/shard_map/all_to_all | solution.py:24
  104.3 32.0 %all-to-all-start.3 = ((f32[128,1,128]{2,1,0:T(1,128)}), f32[128,1,128]{2,1,0:T(1,128)S(1)}, u32[]{:S(2)}, u32[]{:S(2)}) async-start(f32[128,1,128]{2,1,0:T(1,128)} %bitcast.21), calls=%async_computation.3 | async-start | bytes 131072 | tf_op jit(solution)/shard_map/all_to_all | solution.py:18
  137.1 31.3 %all-to-all-start.4 = ((f32[128,1,128]{2,1,0:T(1,128)}), f32[128,1,128]{2,1,0:T(1,128)S(1)}, u32[]{:S(2)}, u32[]{:S(2)}) async-start(f32[128,1,128]{2,1,0:T(1,128)} %bitcast.24), calls=%async_computation.4 | async-start | bytes 131072 | tf_op jit(solution)/shard_map/all_to_all | solution.py:24

commit v6 on v5

--- a/solution.py
+++ b/solution.py
@@ -62,7 +62,7 @@
     square_local = jnp.sum(flat * flat, axis=1)
     upstream = cotangent.astype(jnp.float32) * gain
     inner_local = jnp.sum(upstream * flat, axis=1)
-    square_all, inner_all = head_sum(jnp.stack([square_local, inner_local]), "head")
+    square_all, inner_all = head_sum(jnp.stack([square_local, inner_local]), ("head_cores", "head_chips"))
     recip = lax.rsqrt(square_all / width_all + EPS)
     normed = (flat * recip[:, None] * gain).astype(jnp.bfloat16)
     grad_flat = (
@@ -99,18 +99,20 @@
     )
 
 
-def ctx_split(mesh):
-    ctx_devices = mesh.devices[:, 0]
-    rows_n = len({device.coords[1] for device in ctx_devices})
-    return rows_n, len(ctx_devices) // rows_n
+def axis_split(devices, coord):
+    first = len({device.coords[coord] for device in devices})
+    return first, len(devices) // first
 
 
 def solution(mesh):
-    rows_n, cols_n = ctx_split(mesh)
-    heads_n = mesh.devices.shape[1]
-    split = Mesh(mesh.devices.reshape(rows_n, cols_n, heads_n), ("ctx_rows", "ctx_cols", "head"))
-    rows = P(("ctx_rows", "ctx_cols"), "head")
-    placed = (rows, rows, rows, P("head"), rows)
+    rows_n, cols_n = axis_split(mesh.devices[:, 0], 1)
+    chips_n, cores_n = axis_split(mesh.devices[0, :], 0)
+    split = Mesh(
+        mesh.devices.reshape(rows_n, cols_n, chips_n, cores_n),
+        ("ctx_rows", "ctx_cols", "head_chips", "head_cores"),
+    )
+    rows = P(("ctx_rows", "ctx_cols"), ("head_chips", "head_cores"))
+    placed = (rows, rows, rows, P(("head_chips", "head_cores")), rows)
     return jax.shard_map(
         on_device,
         mesh=split,

time: 171 us -> 171 us (level)
  no operation moved by 1% of the time
where the time goes in v6:
time: 171 us
  waiting for transfers between devices  98.5 us (58%)
  starting transfers between devices  50.7 us (30%)
  blocking collectives  9.37 us (5%)
  local copies, waits for them, and re-layouts  7.3 us (4%)
  matrix products  3.9 us (2%)
    all_to_all x2, waiting for transfers between devices, prefix(): mine = lax.all_to_all(rows, (cols_axis, rows_axis), 0, 0, tiled=True)  50.4 us
    all_to_all x2, waiting for transfers between devices, prefix(): back = lax.all_to_all(total, (cols_axis, rows_axis), 0, 0, tiled=True)  48.1 us
    all_to_all x2, starting transfers between devices, prefix(): mine = lax.all_to_all(rows, (cols_axis, rows_axis), 0, 0, tiled=True)  38.6 us
    all_to_all x2, starting transfers between devices, prefix(): back = lax.all_to_all(total, (cols_axis, rows_axis), 0, 0, tiled=True)  12 us
    all_to_all x1, blocking collectives, head_sum(): gathered = lax.all_to_all(spread, axis, 0, 0, tiled=True)  9.37 us
    unnamed x16, local copies, waits for them, and re-layouts  5.56 us
  transfers between devices with their start and end apart: 4, of which 4 were waited for; matrix products, arithmetic and copies ran while one was open for 2% of the time, Pallas kernels for 0%

profile of v6, /device:TPU:32, one launch (start us, length us, event | category | flops | bytes accessed | tf_op | source)
XLA Modules:
  0.0 170.9 jit_solution(11927320038037263246)
XLA Ops:
  0.6 1.0 copy.75
  1.9 0.7 all_to_all.35
  2.6 32.6 %all-to-all-start = ((f32[128,1,128]{2,1,0:T(1,128)}), f32[128,1,128]{2,1,0:T(1,128)S(1)}, u32[]{:S(2)}, u32[]{:S(2)}) async-start(f32[128,1,128]{2,1,0:T(1,128)} %bitcast.4), calls=%async_computation | async-start | bytes 131072 | tf_op jit(solution)/shard_map/all_to_all | solution.py:18
  35.3 0.7 copy-done.2
  36.2 0.5 copy-done.3
  36.7 24.4 %all-to-all-done = f32[128,1,128]{2,1,0:T(1,128)S(1)} async-done(((f32[128,1,128]{2,1,0:T(1,128)}), f32[128,1,128]{2,1,0:T(1,128)S(1)}, u32[]{:S(2)}, u32[]{:S(2)}) %all-to-all-start) | async-done | bytes 65568 | tf_op jit(solution)/shard_map/all_to_all | solution.py:18
  61.1 0.9 fusion.15
  62.0 6.0 %all-to-all-start.1 = ((f32[128,1,128]{2,1,0:T(1,128)}), f32[128,1,128]{2,1,0:T(1,128)S(1)}, u32[]{:S(2)}, u32[]{:S(2)}) async-start(f32[128,1,128]{2,1,0:T(1,128)} %bitcast.7), calls=%async_computation.1 | async-start | bytes 131072 | tf_op jit(solution)/shard_map/all_to_all | solution.py:24
  68.0 0.2 fusion
  68.4 24.8 %all-to-all-done.1 = f32[128,1,128]{2,1,0:T(1,128)S(1)} async-done(((f32[128,1,128]{2,1,0:T(1,128)}), f32[128,1,128]{2,1,0:T(1,128)S(1)}, u32[]{:S(2)}, u32[]{:S(2)}) %all-to-all-start.1) | async-done | bytes 65568 | tf_op jit(solution)/shard_map/all_to_all | solution.py:24
  93.3 0.2 multiply_reduce_fusion
  93.7 9.4 %all_to_all.53 = f32[8,2,128]{2,1,0:T(2,128)S(1)} all-to-all(f32[8,2,128]{2,1,0:T(2,128)S(1)} %broadcast_in_dim.22), channel_id=1, replica_groups=mesh['ctx_rows'=4,'ctx_cols'=32,'head_chips'=4,'head_cores'=2] {'head_co..., dimensions={0} | all-to-all | bytes 16384 | tf_op jit(solution)/shard_map/all_to_all | solution.py:31
  103.5 0.7 all_to_all.42
  104.2 6.1 %all-to-all-start.3 = ((f32[128,1,128]{2,1,0:T(1,128)}), f32[128,1,128]{2,1,0:T(1,128)S(1)}, u32[]{:S(2)}, u32[]{:S(2)}) async-start(f32[128,1,128]{2,1,0:T(1,128)} %bitcast.21), calls=%async_computation.3 | async-start | bytes 131072 | tf_op jit(solution)/shard_map/all_to_all | solution.py:18
  110.3 0.2 fusion.1
  110.6 26.0 %all-to-all-done.3 = f32[128,1,128]{2,1,0:T(1,128)S(1)} async-done(((f32[128,1,128]{2,1,0:T(1,128)}), f32[128,1,128]{2,1,0:T(1,128)S(1)}, u32[]{:S(2)}, u32[]{:S(2)}) %all-to-all-start.3) | async-done | bytes 65568 | tf_op jit(solution)/shard_map/all_to_all | solution.py:18
  136.5 0.9 fusion.13
  137.4 6.0 %all-to-all-start.4 = ((f32[128,1,128]{2,1,0:T(1,128)}), f32[128,1,128]{2,1,0:T(1,128)S(1)}, u32[]{:S(2)}, u32[]{:S(2)}) async-start(f32[128,1,128]{2,1,0:T(1,128)} %bitcast.24), calls=%async_computation.4 | async-start | bytes 131072 | tf_op jit(solution)/shard_map/all_to_all | solution.py:24
  143.8 0.7 copy.87
  144.5 0.7 copy.86
  145.4 23.4 %all-to-all-done.4 = f32[128,1,128]{2,1,0:T(1,128)S(1)} async-done(((f32[128,1,128]{2,1,0:T(1,128)}), f32[128,1,128]{2,1,0:T(1,128)S(1)}, u32[]{:S(2)}, u32[]{:S(2)}) %all-to-all-start.4) | async-done | bytes 65568 | tf_op jit(solution)/shard_map/all_to_all | solution.py:24
  169.0 0.2 fusion.6
  169.2 0.7 copy.89
  170.1 0.8 copy.88
  (32 shorter events, 2.2 us)
Async XLA Ops:
  0.6 1.0 copy-start
  2.6 32.6 %copy-start.1 = (bf16[128,256]{1,0:T(8,128)(2,1)S(1)}, bf16[128,256]{1,0:T(8,128)(2,1)}, u32[]{:S(2)}) copy-start(bf16[128,256]{1,0:T(8,128)(2,1)} %param.5) | copy-start | bytes 196612
  2.6 58.5 %all-to-all-start = ((f32[128,1,128]{2,1,0:T(1,128)}), f32[128,1,128]{2,1,0:T(1,128)S(1)}, u32[]{:S(2)}, u32[]{:S(2)}) async-start(f32[128,1,128]{2,1,0:T(1,128)} %bitcast.4), calls=%async_computation | async-start | bytes 131072 | tf_op jit(solution)/shard_map/all_to_all | solution.py:18
  35.2 0.8 copy-start.2
  36.1 0.7 copy-start.3
  62.0 31.3 %all-to-all-start.1 = ((f32[128,1,128]{2,1,0:T(1,128)}), f32[128,1,128]{2,1,0:T(1,128)S(1)}, u32[]{:S(2)}, u32[]{:S(2)}) async-start(f32[128,1,128]{2,1,0:T(1,128)} %bitcast.7), calls=%async_computation.1 | async-start | bytes 131072 | tf_op jit(solution)/shard_map/all_to_all | solution.py:24
  104.2 32.3 %all-to-all-start.3 = ((f32[128,1,128]{2,1,0:T(1,128)}), f32[128,1,128]{2,1,0:T(1,128)S(1)}, u32[]{:S(2)}, u32[]{:S(2)}) async-start(f32[128,1,128]{2,1,0:T(1,128)} %bitcast.21), calls=%async_computation.3 | async-start | bytes 131072 | tf_op jit(solution)/shard_map/all_to_all | solution.py:18
  137.4 31.4 %all-to-all-start.4 = ((f32[128,1,128]{2,1,0:T(1,128)}), f32[128,1,128]{2,1,0:T(1,128)S(1)}, u32[]{:S(2)}, u32[]{:S(2)}) async-start(f32[128,1,128]{2,1,0:T(1,128)} %bitcast.24), calls=%async_computation.4 | async-start | bytes 131072 | tf_op jit(solution)/shard_map/all_to_all | solution.py:24

commit v7 on v5

--- a/solution.py
+++ b/solution.py
@@ -10,18 +10,32 @@
 EPS = 1e-05
 
 
-def prefix(value, axes, reverse):
-    rows_axis, cols_axis = axes
-    rows_n, cols_n = lax.axis_size(rows_axis), lax.axis_size(cols_axis)
-    peers = rows_n * cols_n
+CTX_AXES = ("ctx_rows", "ctx_hi", "ctx_lo")
+PEER_AXES = ("ctx_lo", "ctx_hi", "ctx_rows")
+
+
+def ctx_of_peer(peers):
+    sizes = {axis: lax.axis_size(axis) for axis in CTX_AXES}
+    slot = lax.broadcasted_iota(jnp.int32, (peers,), 0)
+    place = {}
+    for axis in reversed(PEER_AXES):
+        place[axis] = slot % sizes[axis]
+        slot = slot // sizes[axis]
+    index = jnp.zeros((peers,), jnp.int32)
+    for axis in CTX_AXES:
+        index = index * sizes[axis] + place[axis]
+    return index
+
+
+def prefix(value, reverse):
+    peers = lax.axis_size(CTX_AXES)
     rows = value.reshape(peers, -1)
-    mine = lax.all_to_all(rows, (cols_axis, rows_axis), 0, 0, tiled=True)
-    slot = lax.broadcasted_iota(jnp.int32, (peers,), 0)
-    order = (slot % rows_n) * cols_n + slot // rows_n
+    mine = lax.all_to_all(rows, PEER_AXES, 0, 0, tiled=True)
+    order = ctx_of_peer(peers)
     row, col = order[:, None], order[None, :]
     before = (col > row) if reverse else (col < row)
     total = jnp.dot(before.astype(mine.dtype), mine, precision=lax.Precision.HIGHEST)
-    back = lax.all_to_all(total, (cols_axis, rows_axis), 0, 0, tiled=True)
+    back = lax.all_to_all(total, PEER_AXES, 0, 0, tiled=True)
     return lax.optimization_barrier(back).reshape(value.shape)
 
 
@@ -50,7 +64,7 @@
     local_state = jnp.einsum(
         "thd,the->hde", key_local, value_local, preferred_element_type=jnp.float32
     )
-    carried = prefix(local_state, ("ctx_rows", "ctx_cols"), False)
+    carried = prefix(local_state, False)
     carried_bf = carried.astype(jnp.bfloat16)
     scores = jnp.einsum("thd,shd->hts", queries, key_local, preferred_element_type=jnp.float32)
     masked = jnp.where(causal[None], scores, 0.0).astype(jnp.bfloat16)
@@ -80,7 +94,7 @@
         "the,hde->thd", grad_out, carried_bf, preferred_element_type=jnp.float32
     )
     local_grad = jnp.einsum("thd,the->hde", queries, grad_out, preferred_element_type=jnp.float32)
-    later = prefix(local_grad, ("ctx_rows", "ctx_cols"), True)
+    later = prefix(local_grad, True)
     later_bf = later.astype(jnp.bfloat16)
     key_grad = jnp.einsum("hts,thd->shd", grad_masked, queries, preferred_element_type=jnp.float32)
     key_grad = key_grad + jnp.einsum(
@@ -102,14 +116,14 @@
 def ctx_split(mesh):
     ctx_devices = mesh.devices[:, 0]
     rows_n = len({device.coords[1] for device in ctx_devices})
-    return rows_n, len(ctx_devices) // rows_n
+    cols_n = len(ctx_devices) // rows_n
+    return rows_n, 2, cols_n // 2
 
 
 def solution(mesh):
-    rows_n, cols_n = ctx_split(mesh)
     heads_n = mesh.devices.shape[1]
-    split = Mesh(mesh.devices.reshape(rows_n, cols_n, heads_n), ("ctx_rows", "ctx_cols", "head"))
-    rows = P(("ctx_rows", "ctx_cols"), "head")
+    split = Mesh(mesh.devices.reshape(ctx_split(mesh) + (heads_n,)), CTX_AXES + ("head",))
+    rows = P(CTX_AXES, "head")
     placed = (rows, rows, rows, P("head"), rows)
     return jax.shard_map(
         on_device,

time: 171 us -> 171 us (level)
  no operation moved by 1% of the time
where the time goes in v7:
time: 171 us; the launch traced here: 170 us
  waiting for transfers between devices  96.8 us (57%)
  starting transfers between devices  51.7 us (30%)
  blocking collectives  9.41 us (6%)
  local copies, waits for them, and re-layouts  7.3 us (4%)
  matrix products  3.91 us (2%)
    all_to_all x2, waiting for transfers between devices, prefix(): mine = lax.all_to_all(rows, PEER_AXES, 0, 0, tiled=True)  49.4 us
    all_to_all x2, waiting for transfers between devices, prefix(): back = lax.all_to_all(total, PEER_AXES, 0, 0, tiled=True)  47.4 us
    all_to_all x2, starting transfers between devices, prefix(): mine = lax.all_to_all(rows, PEER_AXES, 0, 0, tiled=True)  38.9 us
    all_to_all x2, starting transfers between devices, prefix(): back = lax.all_to_all(total, PEER_AXES, 0, 0, tiled=True)  12.7 us
    all_to_all x1, blocking collectives, head_sum(): gathered = lax.all_to_all(spread, axis, 0, 0, tiled=True)  9.41 us
    unnamed x16, local copies, waits for them, and re-layouts  5.56 us
  transfers between devices with their start and end apart: 4, of which 4 were waited for; matrix products, arithmetic and copies ran while one was open for 2% of the time, Pallas kernels for 0%

profile of v7, /device:TPU:32, one launch (start us, length us, event | category | flops | bytes accessed | tf_op | source)
XLA Modules:
  0.0 170.2 jit_solution(271592685239301875)
XLA Ops:
  0.6 1.0 copy.75
  1.9 0.7 all_to_all.35
  2.6 32.6 %all-to-all-start = ((f32[128,1,128]{2,1,0:T(1,128)}), f32[128,1,128]{2,1,0:T(1,128)S(1)}, u32[]{:S(2)}, u32[]{:S(2)}) async-start(f32[128,1,128]{2,1,0:T(1,128)} %bitcast.4), calls=%async_computation | async-start | bytes 131072 | tf_op jit(solution)/shard_map/all_to_all | solution.py:33
  35.3 0.7 copy-done.2
  36.2 0.5 copy-done.3
  36.7 24.0 %all-to-all-done = f32[128,1,128]{2,1,0:T(1,128)S(1)} async-done(((f32[128,1,128]{2,1,0:T(1,128)}), f32[128,1,128]{2,1,0:T(1,128)S(1)}, u32[]{:S(2)}, u32[]{:S(2)}) %all-to-all-start) | async-done | bytes 65568 | tf_op jit(solution)/shard_map/all_to_all | solution.py:33
  60.8 0.9 fusion.15
  61.6 6.4 %all-to-all-start.1 = ((f32[128,1,128]{2,1,0:T(1,128)}), f32[128,1,128]{2,1,0:T(1,128)S(1)}, u32[]{:S(2)}, u32[]{:S(2)}) async-start(f32[128,1,128]{2,1,0:T(1,128)} %bitcast.7), calls=%async_computation.1 | async-start | bytes 131072 | tf_op jit(solution)/shard_map/all_to_all | solution.py:38
  68.0 0.2 fusion
  68.5 24.5 %all-to-all-done.1 = f32[128,1,128]{2,1,0:T(1,128)S(1)} async-done(((f32[128,1,128]{2,1,0:T(1,128)}), f32[128,1,128]{2,1,0:T(1,128)S(1)}, u32[]{:S(2)}, u32[]{:S(2)}) %all-to-all-start.1) | async-done | bytes 65568 | tf_op jit(solution)/shard_map/all_to_all | solution.py:38
  93.0 0.2 multiply_reduce_fusion
  93.4 9.4 %all_to_all.53 = f32[8,2,128]{2,1,0:T(2,128)S(1)} all-to-all(f32[8,2,128]{2,1,0:T(2,128)S(1)} %broadcast_in_dim.22), channel_id=1, replica_groups=mesh['ctx_rows'=4,'ctx_hi'=2,'ctx_lo'=16,'head'=8] {'head'}, dimensions={0} | all-to-all | bytes 16384 | tf_op jit(solution)/shard_map/all_to_all | solution.py:45
  103.2 0.7 all_to_all.42
  104.0 6.4 %all-to-all-start.3 = ((f32[128,1,128]{2,1,0:T(1,128)}), f32[128,1,128]{2,1,0:T(1,128)S(1)}, u32[]{:S(2)}, u32[]{:S(2)}) async-start(f32[128,1,128]{2,1,0:T(1,128)} %bitcast.21), calls=%async_computation.3 | async-start | bytes 131072 | tf_op jit(solution)/shard_map/all_to_all | solution.py:33
  110.4 0.2 fusion.1
  110.6 25.3 %all-to-all-done.3 = f32[128,1,128]{2,1,0:T(1,128)S(1)} async-done(((f32[128,1,128]{2,1,0:T(1,128)}), f32[128,1,128]{2,1,0:T(1,128)S(1)}, u32[]{:S(2)}, u32[]{:S(2)}) %all-to-all-start.3) | async-done | bytes 65568 | tf_op jit(solution)/shard_map/all_to_all | solution.py:33
  135.9 0.9 fusion.13
  136.8 6.3 %all-to-all-start.4 = ((f32[128,1,128]{2,1,0:T(1,128)}), f32[128,1,128]{2,1,0:T(1,128)S(1)}, u32[]{:S(2)}, u32[]{:S(2)}) async-start(f32[128,1,128]{2,1,0:T(1,128)} %bitcast.24), calls=%async_computation.4 | async-start | bytes 131072 | tf_op jit(solution)/shard_map/all_to_all | solution.py:38
  143.5 0.7 copy.87
  144.2 0.7 copy.86
  145.1 22.9 %all-to-all-done.4 = f32[128,1,128]{2,1,0:T(1,128)S(1)} async-done(((f32[128,1,128]{2,1,0:T(1,128)}), f32[128,1,128]{2,1,0:T(1,128)S(1)}, u32[]{:S(2)}, u32[]{:S(2)}) %all-to-all-start.4) | async-done | bytes 65568 | tf_op jit(solution)/shard_map/all_to_all | solution.py:38
  168.3 0.2 fusion.6
  168.5 0.7 copy.89
  169.4 0.8 copy.88
  (32 shorter events, 2.2 us)
Async XLA Ops:
  0.6 1.0 copy-start
  2.6 32.6 %copy-start.1 = (bf16[128,256]{1,0:T(8,128)(2,1)S(1)}, bf16[128,256]{1,0:T(8,128)(2,1)}, u32[]{:S(2)}) copy-start(bf16[128,256]{1,0:T(8,128)(2,1)} %param.5) | copy-start | bytes 196612
  2.6 58.1 %all-to-all-start = ((f32[128,1,128]{2,1,0:T(1,128)}), f32[128,1,128]{2,1,0:T(1,128)S(1)}, u32[]{:S(2)}, u32[]{:S(2)}) async-start(f32[128,1,128]{2,1,0:T(1,128)} %bitcast.4), calls=%async_computation | async-start | bytes 131072 | tf_op jit(solution)/shard_map/all_to_all | solution.py:33
  35.2 0.8 copy-start.2
  36.1 0.7 copy-start.3
  61.6 31.3 %all-to-all-start.1 = ((f32[128,1,128]{2,1,0:T(1,128)}), f32[128,1,128]{2,1,0:T(1,128)S(1)}, u32[]{:S(2)}, u32[]{:S(2)}) async-start(f32[128,1,128]{2,1,0:T(1,128)} %bitcast.7), calls=%async_computation.1 | async-start | bytes 131072 | tf_op jit(solution)/shard_map/all_to_all | solution.py:38
  104.0 32.0 %all-to-all-start.3 = ((f32[128,1,128]{2,1,0:T(1,128)}), f32[128,1,128]{2,1,0:T(1,128)S(1)}, u32[]{:S(2)}, u32[]{:S(2)}) async-start(f32[128,1,128]{2,1,0:T(1,128)} %bitcast.21), calls=%async_computation.3 | async-start | bytes 131072 | tf_op jit(solution)/shard_map/all_to_all | solution.py:33
  136.8 31.3 %all-to-all-start.4 = ((f32[128,1,128]{2,1,0:T(1,128)}), f32[128,1,128]{2,1,0:T(1,128)S(1)}, u32[]{:S(2)}, u32[]{:S(2)}) async-start(f32[128,1,128]{2,1,0:T(1,128)} %bitcast.24), calls=%async_computation.4 | async-start | bytes 131072 | tf_op jit(solution)/shard_map/all_to_all | solution.py:38

commit v8 on v7

--- a/solution.py
+++ b/solution.py
@@ -117,7 +117,7 @@
     ctx_devices = mesh.devices[:, 0]
     rows_n = len({device.coords[1] for device in ctx_devices})
     cols_n = len(ctx_devices) // rows_n
-    return rows_n, 2, cols_n // 2
+    return rows_n, 4, cols_n // 4
 
 
 def solution(mesh):

time: 171 us -> 171 us (level)
  no operation moved by 1% of the time
where the time goes in v8:
time: 171 us; the launch traced here: 170 us
  waiting for transfers between devices  97.3 us (57%)
  starting transfers between devices  51.1 us (30%)
  blocking collectives  9.41 us (6%)
  local copies, waits for them, and re-layouts  7.3 us (4%)
  matrix products  3.9 us (2%)
    all_to_all x2, waiting for transfers between devices, prefix(): mine = lax.all_to_all(rows, PEER_AXES, 0, 0, tiled=True)  49.6 us
    all_to_all x2, waiting for transfers between devices, prefix(): back = lax.all_to_all(total, PEER_AXES, 0, 0, tiled=True)  47.8 us
    all_to_all x2, starting transfers between devices, prefix(): mine = lax.all_to_all(rows, PEER_AXES, 0, 0, tiled=True)  38.7 us
    all_to_all x2, starting transfers between devices, prefix(): back = lax.all_to_all(total, PEER_AXES, 0, 0, tiled=True)  12.4 us
    all_to_all x1, blocking collectives, head_sum(): gathered = lax.all_to_all(spread, axis, 0, 0, tiled=True)  9.41 us
    unnamed x16, local copies, waits for them, and re-layouts  5.56 us
  transfers between devices with their start and end apart: 4, of which 4 were waited for; matrix products, arithmetic and copies ran while one was open for 2% of the time, Pallas kernels for 0%

profile of v8, /device:TPU:32, one launch (start us, length us, event | category | flops | bytes accessed | tf_op | source)
XLA Modules:
  0.0 170.2 jit_solution(14239372334080661924)
XLA Ops:
  0.6 1.0 copy.75
  1.9 0.7 all_to_all.35
  2.6 32.6 %all-to-all-start = ((f32[128,1,128]{2,1,0:T(1,128)}), f32[128,1,128]{2,1,0:T(1,128)S(1)}, u32[]{:S(2)}, u32[]{:S(2)}) async-start(f32[128,1,128]{2,1,0:T(1,128)} %bitcast.4), calls=%async_computation | async-start | bytes 131072 | tf_op jit(solution)/shard_map/all_to_all | solution.py:33
  35.3 0.7 copy-done.2
  36.2 0.5 copy-done.3
  36.7 24.1 %all-to-all-done = f32[128,1,128]{2,1,0:T(1,128)S(1)} async-done(((f32[128,1,128]{2,1,0:T(1,128)}), f32[128,1,128]{2,1,0:T(1,128)S(1)}, u32[]{:S(2)}, u32[]{:S(2)}) %all-to-all-start) | async-done | bytes 65568 | tf_op jit(solution)/shard_map/all_to_all | solution.py:33
  60.8 0.9 fusion.15
  61.7 6.1 %all-to-all-start.1 = ((f32[128,1,128]{2,1,0:T(1,128)}), f32[128,1,128]{2,1,0:T(1,128)S(1)}, u32[]{:S(2)}, u32[]{:S(2)}) async-start(f32[128,1,128]{2,1,0:T(1,128)} %bitcast.7), calls=%async_computation.1 | async-start | bytes 131072 | tf_op jit(solution)/shard_map/all_to_all | solution.py:38
  67.8 0.2 fusion
  68.3 24.7 %all-to-all-done.1 = f32[128,1,128]{2,1,0:T(1,128)S(1)} async-done(((f32[128,1,128]{2,1,0:T(1,128)}), f32[128,1,128]{2,1,0:T(1,128)S(1)}, u32[]{:S(2)}, u32[]{:S(2)}) %all-to-all-start.1) | async-done | bytes 65568 | tf_op jit(solution)/shard_map/all_to_all | solution.py:38
  93.0 0.2 multiply_reduce_fusion
  93.4 9.4 %all_to_all.53 = f32[8,2,128]{2,1,0:T(2,128)S(1)} all-to-all(f32[8,2,128]{2,1,0:T(2,128)S(1)} %broadcast_in_dim.22), channel_id=1, replica_groups=mesh['ctx_rows'=4,'ctx_hi'=4,'ctx_lo'=8,'head'=8] {'head'}, dimensions={0} | all-to-all | bytes 16384 | tf_op jit(solution)/shard_map/all_to_all | solution.py:45
  103.3 0.7 all_to_all.42
  104.0 6.1 %all-to-all-start.3 = ((f32[128,1,128]{2,1,0:T(1,128)}), f32[128,1,128]{2,1,0:T(1,128)S(1)}, u32[]{:S(2)}, u32[]{:S(2)}) async-start(f32[128,1,128]{2,1,0:T(1,128)} %bitcast.21), calls=%async_computation.3 | async-start | bytes 131072 | tf_op jit(solution)/shard_map/all_to_all | solution.py:33
  110.1 0.2 fusion.1
  110.4 25.5 %all-to-all-done.3 = f32[128,1,128]{2,1,0:T(1,128)S(1)} async-done(((f32[128,1,128]{2,1,0:T(1,128)}), f32[128,1,128]{2,1,0:T(1,128)S(1)}, u32[]{:S(2)}, u32[]{:S(2)}) %all-to-all-start.3) | async-done | bytes 65568 | tf_op jit(solution)/shard_map/all_to_all | solution.py:33
  135.8 0.9 fusion.13
  136.7 6.3 %all-to-all-start.4 = ((f32[128,1,128]{2,1,0:T(1,128)}), f32[128,1,128]{2,1,0:T(1,128)S(1)}, u32[]{:S(2)}, u32[]{:S(2)}) async-start(f32[128,1,128]{2,1,0:T(1,128)} %bitcast.24), calls=%async_computation.4 | async-start | bytes 131072 | tf_op jit(solution)/shard_map/all_to_all | solution.py:38
  143.3 0.7 copy.87
  144.1 0.7 copy.86
  145.0 23.1 %all-to-all-done.4 = f32[128,1,128]{2,1,0:T(1,128)S(1)} async-done(((f32[128,1,128]{2,1,0:T(1,128)}), f32[128,1,128]{2,1,0:T(1,128)S(1)}, u32[]{:S(2)}, u32[]{:S(2)}) %all-to-all-start.4) | async-done | bytes 65568 | tf_op jit(solution)/shard_map/all_to_all | solution.py:38
  168.3 0.2 fusion.6
  168.5 0.7 copy.89
  169.4 0.8 copy.88
  (32 shorter events, 2.2 us)
Async XLA Ops:
  0.6 1.0 copy-start
  2.6 32.6 %copy-start.1 = (bf16[128,256]{1,0:T(8,128)(2,1)S(1)}, bf16[128,256]{1,0:T(8,128)(2,1)}, u32[]{:S(2)}) copy-start(bf16[128,256]{1,0:T(8,128)(2,1)} %param.5) | copy-start | bytes 196612
  2.6 58.2 %all-to-all-start = ((f32[128,1,128]{2,1,0:T(1,128)}), f32[128,1,128]{2,1,0:T(1,128)S(1)}, u32[]{:S(2)}, u32[]{:S(2)}) async-start(f32[128,1,128]{2,1,0:T(1,128)} %bitcast.4), calls=%async_computation | async-start | bytes 131072 | tf_op jit(solution)/shard_map/all_to_all | solution.py:33
  35.2 0.8 copy-start.2
  36.1 0.7 copy-start.3
  61.7 31.2 %all-to-all-start.1 = ((f32[128,1,128]{2,1,0:T(1,128)}), f32[128,1,128]{2,1,0:T(1,128)S(1)}, u32[]{:S(2)}, u32[]{:S(2)}) async-start(f32[128,1,128]{2,1,0:T(1,128)} %bitcast.7), calls=%async_computation.1 | async-start | bytes 131072 | tf_op jit(solution)/shard_map/all_to_all | solution.py:38
  104.0 31.8 %all-to-all-start.3 = ((f32[128,1,128]{2,1,0:T(1,128)}), f32[128,1,128]{2,1,0:T(1,128)S(1)}, u32[]{:S(2)}, u32[]{:S(2)}) async-start(f32[128,1,128]{2,1,0:T(1,128)} %bitcast.21), calls=%async_computation.3 | async-start | bytes 131072 | tf_op jit(solution)/shard_map/all_to_all | solution.py:33
  136.7 31.4 %all-to-all-start.4 = ((f32[128,1,128]{2,1,0:T(1,128)}), f32[128,1,128]{2,1,0:T(1,128)S(1)}, u32[]{:S(2)}, u32[]{:S(2)}) async-start(f32[128,1,128]{2,1,0:T(1,128)} %bitcast.24), calls=%async_computation.4 | async-start | bytes 131072 | tf_op jit(solution)/shard_map/all_to_all | solution.py:38

commit v9 on v7

--- a/solution.py
+++ b/solution.py
@@ -11,7 +11,7 @@
 
 
 CTX_AXES = ("ctx_rows", "ctx_hi", "ctx_lo")
-PEER_AXES = ("ctx_lo", "ctx_hi", "ctx_rows")
+PEER_AXES = ("ctx_lo", "ctx_rows", "ctx_hi")
 
 
 def ctx_of_peer(peers):

time: 171 us -> 171 us (level)
  no operation moved by 1% of the time
where the time goes in v9:
time: 171 us
  waiting for transfers between devices  98.5 us (58%)
  starting transfers between devices  50.5 us (30%)
  blocking collectives  9.41 us (6%)
  local copies, waits for them, and re-layouts  7.3 us (4%)
  matrix products  3.9 us (2%)
    all_to_all x2, waiting for transfers between devices, prefix(): mine = lax.all_to_all(rows, PEER_AXES, 0, 0, tiled=True)  50.2 us
    all_to_all x2, waiting for transfers between devices, prefix(): back = lax.all_to_all(total, PEER_AXES, 0, 0, tiled=True)  48.3 us
    all_to_all x2, starting transfers between devices, prefix(): mine = lax.all_to_all(rows, PEER_AXES, 0, 0, tiled=True)  38.5 us
    all_to_all x2, starting transfers between devices, prefix(): back = lax.all_to_all(total, PEER_AXES, 0, 0, tiled=True)  11.9 us
    all_to_all x1, blocking collectives, head_sum(): gathered = lax.all_to_all(spread, axis, 0, 0, tiled=True)  9.41 us
    unnamed x16, local copies, waits for them, and re-layouts  5.56 us
  transfers between devices with their start and end apart: 4, of which 4 were waited for; matrix products, arithmetic and copies ran while one was open for 2% of the time, Pallas kernels for 0%

profile of v9, /device:TPU:32, one launch (start us, length us, event | category | flops | bytes accessed | tf_op | source)
XLA Modules:
  0.0 170.7 jit_solution(11212746798943313418)
XLA Ops:
  0.6 1.0 copy.75
  1.9 0.7 all_to_all.35
  2.6 32.6 %all-to-all-start = ((f32[128,1,128]{2,1,0:T(1,128)}), f32[128,1,128]{2,1,0:T(1,128)S(1)}, u32[]{:S(2)}, u32[]{:S(2)}) async-start(f32[128,1,128]{2,1,0:T(1,128)} %bitcast.4), calls=%async_computation | async-start | bytes 131072 | tf_op jit(solution)/shard_map/all_to_all | solution.py:33
  35.3 0.7 copy-done.2
  36.2 0.5 copy-done.3
  36.7 24.5 %all-to-all-done = f32[128,1,128]{2,1,0:T(1,128)S(1)} async-done(((f32[128,1,128]{2,1,0:T(1,128)}), f32[128,1,128]{2,1,0:T(1,128)S(1)}, u32[]{:S(2)}, u32[]{:S(2)}) %all-to-all-start) | async-done | bytes 65568 | tf_op jit(solution)/shard_map/all_to_all | solution.py:33
  61.2 0.9 fusion.15
  62.1 6.0 %all-to-all-start.1 = ((f32[128,1,128]{2,1,0:T(1,128)}), f32[128,1,128]{2,1,0:T(1,128)S(1)}, u32[]{:S(2)}, u32[]{:S(2)}) async-start(f32[128,1,128]{2,1,0:T(1,128)} %bitcast.7), calls=%async_computation.1 | async-start | bytes 131072 | tf_op jit(solution)/shard_map/all_to_all | solution.py:38
  68.1 0.2 fusion
  68.5 24.9 %all-to-all-done.1 = f32[128,1,128]{2,1,0:T(1,128)S(1)} async-done(((f32[128,1,128]{2,1,0:T(1,128)}), f32[128,1,128]{2,1,0:T(1,128)S(1)}, u32[]{:S(2)}, u32[]{:S(2)}) %all-to-all-start.1) | async-done | bytes 65568 | tf_op jit(solution)/shard_map/all_to_all | solution.py:38
  93.5 0.2 multiply_reduce_fusion
  93.9 9.4 %all_to_all.53 = f32[8,2,128]{2,1,0:T(2,128)S(1)} all-to-all(f32[8,2,128]{2,1,0:T(2,128)S(1)} %broadcast_in_dim.22), channel_id=1, replica_groups=mesh['ctx_rows'=4,'ctx_hi'=2,'ctx_lo'=16,'head'=8] {'head'}, dimensions={0} | all-to-all | bytes 16384 | tf_op jit(solution)/shard_map/all_to_all | solution.py:45
  103.7 0.7 all_to_all.42
  104.4 6.0 %all-to-all-start.3 = ((f32[128,1,128]{2,1,0:T(1,128)}), f32[128,1,128]{2,1,0:T(1,128)S(1)}, u32[]{:S(2)}, u32[]{:S(2)}) async-start(f32[128,1,128]{2,1,0:T(1,128)} %bitcast.21), calls=%async_computation.3 | async-start | bytes 131072 | tf_op jit(solution)/shard_map/all_to_all | solution.py:33
  110.4 0.2 fusion.1
  110.6 25.7 %all-to-all-done.3 = f32[128,1,128]{2,1,0:T(1,128)S(1)} async-done(((f32[128,1,128]{2,1,0:T(1,128)}), f32[128,1,128]{2,1,0:T(1,128)S(1)}, u32[]{:S(2)}, u32[]{:S(2)}) %all-to-all-start.3) | async-done | bytes 65568 | tf_op jit(solution)/shard_map/all_to_all | solution.py:33
  136.4 0.9 fusion.13
  137.2 6.0 %all-to-all-start.4 = ((f32[128,1,128]{2,1,0:T(1,128)}), f32[128,1,128]{2,1,0:T(1,128)S(1)}, u32[]{:S(2)}, u32[]{:S(2)}) async-start(f32[128,1,128]{2,1,0:T(1,128)} %bitcast.24), calls=%async_computation.4 | async-start | bytes 131072 | tf_op jit(solution)/shard_map/all_to_all | solution.py:38
  143.6 0.7 copy.87
  144.3 0.7 copy.86
  145.2 23.4 %all-to-all-done.4 = f32[128,1,128]{2,1,0:T(1,128)S(1)} async-done(((f32[128,1,128]{2,1,0:T(1,128)}), f32[128,1,128]{2,1,0:T(1,128)S(1)}, u32[]{:S(2)}, u32[]{:S(2)}) %all-to-all-start.4) | async-done | bytes 65568 | tf_op jit(solution)/shard_map/all_to_all | solution.py:38
  168.8 0.2 fusion.6
  169.0 0.7 copy.89
  169.9 0.8 copy.88
  (32 shorter events, 2.2 us)
Async XLA Ops:
  0.6 1.0 copy-start
  2.6 32.6 %copy-start.1 = (bf16[128,256]{1,0:T(8,128)(2,1)S(1)}, bf16[128,256]{1,0:T(8,128)(2,1)}, u32[]{:S(2)}) copy-start(bf16[128,256]{1,0:T(8,128)(2,1)} %param.5) | copy-start | bytes 196612
  2.6 58.6 %all-to-all-start = ((f32[128,1,128]{2,1,0:T(1,128)}), f32[128,1,128]{2,1,0:T(1,128)S(1)}, u32[]{:S(2)}, u32[]{:S(2)}) async-start(f32[128,1,128]{2,1,0:T(1,128)} %bitcast.4), calls=%async_computation | async-start | bytes 131072 | tf_op jit(solution)/shard_map/all_to_all | solution.py:33
  35.2 0.8 copy-start.2
  36.1 0.7 copy-start.3
  62.1 31.3 %all-to-all-start.1 = ((f32[128,1,128]{2,1,0:T(1,128)}), f32[128,1,128]{2,1,0:T(1,128)S(1)}, u32[]{:S(2)}, u32[]{:S(2)}) async-start(f32[128,1,128]{2,1,0:T(1,128)} %bitcast.7), calls=%async_computation.1 | async-start | bytes 131072 | tf_op jit(solution)/shard_map/all_to_all | solution.py:38
  104.4 31.9 %all-to-all-start.3 = ((f32[128,1,128]{2,1,0:T(1,128)}), f32[128,1,128]{2,1,0:T(1,128)S(1)}, u32[]{:S(2)}, u32[]{:S(2)}) async-start(f32[128,1,128]{2,1,0:T(1,128)} %bitcast.21), calls=%async_computation.3 | async-start | bytes 131072 | tf_op jit(solution)/shard_map/all_to_all | solution.py:33
  137.2 31.3 %all-to-all-start.4 = ((f32[128,1,128]{2,1,0:T(1,128)}), f32[128,1,128]{2,1,0:T(1,128)S(1)}, u32[]{:S(2)}, u32[]{:S(2)}) async-start(f32[128,1,128]{2,1,0:T(1,128)} %bitcast.24), calls=%async_computation.4 | async-start | bytes 131072 | tf_op jit(solution)/shard_map/all_to_all | solution.py:38
